TPU v7x, 256 devices: a whole 4x4x8 slice. The times are simulated.
256 devices in a mesh: rep: 32 (over z, y_hi, core), tp: 8 (over x, y_lo).
Axes of the slice: x: 4, y: 4 (y_hi: 2, y_lo: 2; y = y_hi * 2 + y_lo), z: 8, core: 2. Of those that a mesh axis runs over, the one named last changes fastest.
Arguments:
- acts: bfloat16 [32, 1024, 4096], P('rep', 'tp'), may hold values from -6 to 6
- weights: bfloat16 [32, 4096, 4096], P('rep', None, 'tp'), may hold values from -6 to 6
- cotangent: bfloat16 [32, 1024, 4096], P('rep', None, 'tp'), may hold values from -6 to 6
- start_factors: float32 [4096, 32], replicated, may hold values from -6 to 6
Outputs:
- projected: bfloat16 [32, 1024, 4096], P('rep', None, 'tp')
- new_weights: bfloat16 [32, 4096, 4096], P('rep', None, 'tp')
All inputs are finite; a program needn't handle non-finite values.
Results may differ from a plain program's by a relative error of at most 0.001.
Values may be sent and summed in bfloat16 or wider, within the bound.
No kernel may reach another device: no remote copies, remote signals or barrier semaphores. Data moves between devices by JAX's collectives and lax.ppermute only.
A program may use at most 128 MiB of HBM per device.

v0:
```python
import jax
import jax.numpy as jnp
from jax import lax
from jax.sharding import PartitionSpec as P

D = 4096
STEPS = 3


HIGH = lax.Precision.HIGHEST


def partner(block, axis, stride):
    count = lax.axis_size(axis)
    route = []
    for low in range(count):
        high = low | 1 << stride
        if high != low and high < count:
            route += [(low, high), (high, low)]
    return lax.ppermute(block, axis, route)


def shards(acts, weights, cotangent, start_factors):
    scale = D ** (-0.5)
    weight_part = weights[0]
    grad_out = cotangent[0]
    projected = (
        jnp.dot(
            lax.all_gather(acts, "tp", axis=1, tiled=True)[0],
            weight_part,
            preferred_element_type=jnp.float32,
        )
        * scale
    ).astype(jnp.bfloat16)[None]
    grad = lax.dot_general(
        lax.all_gather(acts, "tp", axis=1, tiled=True)[0],
        grad_out,
        (((0,), (0,)), ((), ())),
        preferred_element_type=jnp.float32,
    )
    current = weight_part.astype(jnp.float32) - 0.5 * scale * grad
    for step in range(STEPS):
        side = lax.dot_general(current, start_factors, (((0,), (0,)), ((), ())), precision=HIGH)
        other = partner(side, "rep", step)
        diff = side - other
        gram = lax.psum(jnp.dot(diff.T, diff, precision=HIGH), "tp")
        lower = jnp.linalg.cholesky(gram)
        ortho = jax.scipy.linalg.solve_triangular(lower, diff.T, lower=True).T
        local = jnp.dot(current, ortho, precision=HIGH)
        summed = lax.psum(local, "tp")
        back = summed + partner(summed, "rep", step)
        current = current - 0.5 * jnp.dot(back, ortho.T, precision=HIGH)
    return (projected, current.astype(jnp.bfloat16)[None])


def solution(mesh):
    in_specs = (P("rep", "tp", None), P("rep", None, "tp"), P("rep", None, "tp"), P())
    out_specs = (P("rep", None, "tp"), P("rep", None, "tp"))
    return jax.shard_map(shards, mesh=mesh, in_specs=in_specs, out_specs=out_specs, check_vma=False)
```

profile of v0, /device:TPU:16, one launch (start us, length us, event | category | flops | bytes accessed | tf_op | source)
XLA Modules:
  0.0 682.2 jit_solution(12295986545836351096)
XLA Ops:
  8.0 175.2 %all-gather.2.cloned.1.call-done = bf16[1,1024,4096]{2,1,0:T(8,128)(2,1)} async-done(((bf16[1,128,4096]{2,1,0:T(8,128)(2,1)}), bf16[1,1024,4096]{2,1,0:T(8,128)(2,1)}) %all-gather.2.cloned.1.call-update) | async-done | bytes 8388624 | tf_op jit(solution)/shard_map/all_gather | solution.py:29
  183.2 12.2 %multiply_subtract_fusion.2 = f32[4096,512]{1,0:T(8,128)S(1)} fusion(bf16[1,1024,4096]{2,1,0:T(8,128)(2,1)} %all-gather.2.cloned.1.call-done, bf16[1,4096,512]{2,1,0:T(8,128)(2,1)} %param.8, bf16[1,1024,512]{2,1,0:T(8,128)(2,1)S(1)} %copy-done), kind=kOutput, calls=%fused_computation.7 | convolution fusion | flops 4301258752 | bytes 22020096 | tf_op jit(solution)/shard_map/dot_general | solution.py:35
  195.4 3.2 copy-done.3
  198.6 5.1 fusion.45
  205.2 34.0 %psum.42 = f32[32,32]{0,1:T(8,128)S(1)} all-reduce(f32[32,32]{0,1:T(8,128)S(1)} %fusion.34), channel_id=1, replica_groups=mesh['rep'=32,'tp'=8] {'tp'}, use_global_device_ids=true, to_apply=%region_0.0 | all-reduce | flops 1024 | bytes 8192 | tf_op jit(solution)/shard_map/psum | solution.py:46
  239.4 2.9 cholesky.59
  243.6 2.4 custom-call.7
  246.3 10.8 %fusion.46 = f32[4096,32]{0,1:T(8,128)} fusion(f32[4096,512]{1,0:T(8,128)} %copy-done.3, f32[32,512]{1,0:T(8,128)S(1)} %fusion.25), kind=kOutput, calls=%fused_computation.55 | convolution fusion | flops 805306368 | bytes 8978432 | tf_op jit(solution)/shard_map/dot_general | solution.py:49
  257.2 78.7 %all-reduce.4.cloned.1.call-done = f32[4096,32]{0,1:T(8,128)} async-done(((f32[4096,32]{0,1:T(8,128)}), f32[4096,32]{0,1:T(8,128)}) %all-reduce.4.cloned.1.call-update) | async-done | bytes 524304 | tf_op jit(solution)/shard_map/psum | solution.py:50
  335.9 2.1 collective-permute-done.1
  338.0 9.4 %multiply_subtract_fusion.1 = f32[4096,512]{1,0:T(8,128)S(1)} fusion(f32[4096,512]{1,0:T(8,128)} %copy-done.3, f32[32,512]{1,0:T(8,128)S(1)} %fusion.25, f32[4096,32]{0,1:T(8,128)} %all-reduce.4.cloned.1.call-done, f32[4096,32]{0,1:T(8,128)S(1)} %collective-permute-done.1), kind=kOutput, calls=%fused_computation.6 | convolution fusion | flops 809631744 | bytes 17891328 | tf_op jit(solution)/shard_map/dot_general | solution.py:52
  347.4 3.2 copy-done.1
  350.6 5.1 fusion.47
  356.7 4.9 collective-permute-done.2
  361.8 32.4 %psum.44 = f32[32,32]{0,1:T(8,128)S(1)} all-reduce(f32[32,32]{0,1:T(8,128)S(1)} %fusion.31), channel_id=1, replica_groups=mesh['rep'=32,'tp'=8] {'tp'}, use_global_device_ids=true, to_apply=%region_4.0 | all-reduce | flops 1024 | bytes 8192 | tf_op jit(solution)/shard_map/psum | solution.py:46
  394.3 2.9 cholesky.70
  398.5 2.4 custom-call.8
  401.3 10.8 %fusion.48 = f32[4096,32]{0,1:T(8,128)} fusion(f32[4096,512]{1,0:T(8,128)} %copy-done.1, f32[32,512]{1,0:T(8,128)S(1)} %fusion.23), kind=kOutput, calls=%fused_computation.57 | convolution fusion | flops 805306368 | bytes 8978432 | tf_op jit(solution)/shard_map/dot_general | solution.py:49
  412.1 78.8 %all-reduce.6.cloned.1.call-done = f32[4096,32]{0,1:T(8,128)} async-done(((f32[4096,32]{0,1:T(8,128)}), f32[4096,32]{0,1:T(8,128)}) %all-reduce.6.cloned.1.call-update) | async-done | bytes 524304 | tf_op jit(solution)/shard_map/psum | solution.py:50
  491.8 10.0 %collective-permute-done.3 = f32[4096,32]{0,1:T(8,128)S(1)} collective-permute-done((f32[4096,32]{0,1:T(8,128)}, f32[4096,32]{0,1:T(8,128)S(1)}, u32[]{:S(2)}, u32[]{:S(2)}) %collective-permute-start.3) | collective-permute-done | bytes 524320 | tf_op jit(solution)/shard_map/ppermute | solution.py:20
  501.8 9.4 %multiply_subtract_fusion = f32[4096,512]{1,0:T(8,128)S(1)} fusion(f32[4096,512]{1,0:T(8,128)} %copy-done.1, f32[32,512]{1,0:T(8,128)S(1)} %fusion.23, f32[4096,32]{0,1:T(8,128)} %all-reduce.6.cloned.1.call-done, f32[4096,32]{0,1:T(8,128)S(1)} %collective-permute-done.3), kind=kOutput, calls=%fused_computation.5 | convolution fusion | flops 809631744 | bytes 17891328 | tf_op jit(solution)/shard_map/dot_general | solution.py:52
  511.3 3.2 copy-done.2
  514.5 5.1 fusion.49
  519.5 1.6 collective-permute-start.4
  521.2 2.7 collective-permute-done.4
  524.1 32.5 %psum.46 = f32[32,32]{0,1:T(8,128)S(1)} all-reduce(f32[32,32]{0,1:T(8,128)S(1)} %fusion.28), channel_id=1, replica_groups=mesh['rep'=32,'tp'=8] {'tp'}, use_global_device_ids=true, to_apply=%region_6.9 | all-reduce | flops 1024 | bytes 8192 | tf_op jit(solution)/shard_map/psum | solution.py:46
  556.7 2.9 cholesky.81
  560.9 2.4 custom-call.9
  563.6 10.8 %fusion.50 = f32[4096,32]{0,1:T(8,128)} fusion(f32[4096,512]{1,0:T(8,128)} %copy-done.2, f32[32,512]{1,0:T(8,128)S(1)} %fusion.21), kind=kOutput, calls=%fused_computation.59 | convolution fusion | flops 805306368 | bytes 8978432 | tf_op jit(solution)/shard_map/dot_general | solution.py:49
  574.4 78.8 %all-reduce.8.cloned.1.call-done = f32[4096,32]{0,1:T(8,128)} async-done(((f32[4096,32]{0,1:T(8,128)}), f32[4096,32]{0,1:T(8,128)}) %all-reduce.8.cloned.1.call-update) | async-done | bytes 524304 | tf_op jit(solution)/shard_map/psum | solution.py:50
  654.8 10.0 %fusion.12 = bf16[1,1024,512]{2,1,0:T(8,128)(2,1)} fusion(bf16[1,4096,512]{2,1,0:T(8,128)(2,1)} %param.8, bf16[1,1024,4096]{2,1,0:T(8,128)(2,1)} %all-gather.2.cloned.1.call-done), kind=kOutput, calls=%fused_computation.11 | convolution fusion | flops 4296015872 | bytes 13631488 | tf_op jit(solution)/shard_map/dot_general | solution.py:28
  664.8 10.6 %fusion.6 = bf16[1,4096,512]{2,1,0:T(8,128)(2,1)} fusion(f32[4096,512]{1,0:T(8,128)} %copy-done.2, f32[32,512]{1,0:T(8,128)S(1)} %fusion.21, f32[4096,32]{0,1:T(8,128)S(1)} %copy-done.5, f32[4096,32]{0,1:T(8,128)S(1)} %collective-permute-done.5), kind=kOutput, calls=%fused_computation.8 | convolution fusion | flops 811728896 | bytes 13697024 | tf_op jit(solution)/shard_map/dot_general | solution.py:52
  (45 shorter events, 11.3 us)
Async XLA Ops:
  7.2 176.0 %copy-start = (bf16[1,1024,512]{2,1,0:T(8,128)(2,1)S(1)}, bf16[1,1024,512]{2,1,0:T(8,128)(2,1)}, u32[]{:S(2)}) copy-start(bf16[1,1024,512]{2,1,0:T(8,128)(2,1)} %param.9) | copy-start | bytes 3145732
  7.2 176.0 %all-gather.2.cloned.1.call-start = ((), (), s32[]{:S(2)}) async-start(), calls=%async_computation | async-start | bytes 9437184 | tf_op jit(solution)/shard_map/all_gather | solution.py:29
  7.9 190.7 %copy-start.4 = (f32[4096,32]{0,1:T(8,128)S(1)}, f32[4096,32]{0,1:T(8,128)}, u32[]{:S(2)}) copy-start(f32[4096,32]{0,1:T(8,128)} %param.10) | copy-start | bytes 1572868
  7.9 328.0 %all-reduce.4.cloned.1.call-start = ((), (), s32[]{:S(2)}) async-start(), calls=%async_computation.1 | async-start | bytes 1048576 | tf_op jit(solution)/shard_map/psum | solution.py:50
  195.4 3.2 copy-start.3
  203.7 1.3 collective-permute-start
  257.1 233.8 %all-reduce.6.cloned.1.call-start = ((), (), s32[]{:S(2)}) async-start(), calls=%async_computation.2 | async-start | bytes 1048576 | tf_op jit(solution)/shard_map/psum | solution.py:50
  335.9 2.1 collective-permute-start.1
  347.4 3.2 copy-start.1
  355.7 5.9 collective-permute-start.2
  412.1 241.1 %all-reduce.8.cloned.1.call-start = ((), (), s32[]{:S(2)}) async-start(), calls=%async_computation.3 | async-start | bytes 1048576 | tf_op jit(solution)/shard_map/psum | solution.py:50
  490.9 10.9 %collective-permute-start.3 = (f32[4096,32]{0,1:T(8,128)}, f32[4096,32]{0,1:T(8,128)S(1)}, u32[]{:S(2)}, u32[]{:S(2)}) collective-permute-start(f32[4096,32]{0,1:T(8,128)} %all-reduce.6.cloned.1.call-done), channel_id=1, source_target_pairs={{0,16},{16,0},{8,24},{24,8},{32,48},{48,32},{40,56},{56,40},{64,80... | collective-permute-start | bytes 1572872 | tf_op jit(solution)/shard_map/ppermute | solution.py:20
  511.3 3.2 copy-start.2
  519.5 4.4 collective-permute-start.4
  653.2 11.6 %copy-start.5 = (f32[4096,32]{0,1:T(8,128)S(1)}, f32[4096,32]{0,1:T(8,128)}, u32[]{:S(2)}) copy-start(f32[4096,32]{0,1:T(8,128)} %all-reduce.8.cloned.1.call-done) | copy-start | bytes 1572868
  653.2 11.6 %collective-permute-start.5 = (f32[4096,32]{0,1:T(8,128)}, f32[4096,32]{0,1:T(8,128)S(1)}, u32[]{:S(2)}, u32[]{:S(2)}) collective-permute-start(f32[4096,32]{0,1:T(8,128)} %all-reduce.8.cloned.1.call-done), channel_id=1, source_target_pairs={{0,32},{32,0},{8,40},{40,8},{16,48},{48,16},{24,56},{56,24},{64,96... | collective-permute-start | bytes 1572872 | tf_op jit(solution)/shard_map/ppermute | solution.py:20
Sparse Core Ops, SparseCore 0:
  9.8 173.3 all-gather.1
  257.3 78.5 all-reduce.3
  412.2 78.7 all-reduce.5
  574.6 78.6 all-reduce.7
where the time goes:
time: 689 us; the launch traced here: 682 us
  waiting for transfers between devices  433 us (63%)
  matrix products  101 us (15%)
  blocking collectives  98.9 us (14%)
  other arithmetic  20.1 us (3%)
  between operations  14.2 us (2%)
  local copies, waits for them, and re-layouts  9.85 us (1%)
    psum x3, waiting for transfers between devices, shards(): summed = lax.psum(local, 'tp')  236 us
    all_gather x1, waiting for transfers between devices, shards(): lax.all_gather(acts, 'tp', axis=1, tiled=True)[0]  175 us
    psum x3, blocking collectives, shards(): gram = lax.psum(jnp.dot(diff.T, diff, precision=HIGH), 'tp')  98.9 us
    dot_general x3, matrix products, shards(): local = jnp.dot(current, ortho, precision=HIGH)  32.3 us
    dot_general x3, matrix products, shards(): current = current - 0.5 * jnp.dot(back, ortho.T, precision=HIGH)  29.5 us
    ppermute x6, waiting for transfers between devices, partner(): return lax.ppermute(block, axis, route)  21 us
    dot_general x3, matrix products, shards(): lax.dot_general(current, start_factors, (((0,), (0,)), ((), ())), precisi...  15.2 us
  transfers between devices with their start and end apart: 10, of which 9 were waited for; matrix products, arithmetic and copies ran while one was open for 1% of the time, Pallas kernels for 0%

commit v1 on v0

v1 whole, which is shorter than its diff:
```python
import numpy as np
import jax
import jax.numpy as jnp
from jax import lax
from jax.sharding import Mesh, PartitionSpec as P

D = 4096
STEPS = 3


HIGH = lax.Precision.HIGHEST
F32 = jnp.float32


def swap(block, axis):
    return lax.ppermute(block, axis, [(0, 1), (1, 0)])


def tp_perm(count, fn):
    return [(t, fn(t)) for t in range(count)]


def gather_tokens(own, count):
    if count != 8:
        whole = lax.all_gather(own, "tp", axis=0, tiled=False)
        return [whole[k] for k in range(count)], None
    nx = count // 2

    def shift(d):
        return tp_perm(count, lambda t: ((t // 2 + d) % nx) * 2 + t % 2)

    rows = own.shape[0]
    h = rows // 2
    a_y = lax.ppermute(own, "tp", tp_perm(count, lambda t: t ^ 1))
    a_m = lax.ppermute(own, "tp", shift(1))
    a_p = lax.ppermute(own, "tp", shift(-1))
    r_m = lax.ppermute(jnp.concatenate([a_y, a_m[:h]]), "tp", shift(1))
    r_p = lax.ppermute(jnp.concatenate([a_y, a_p[h:]]), "tp", shift(-1))
    c_m = lax.ppermute(r_m[:h], "tp", shift(1))
    c_p = lax.ppermute(r_p[h:rows], "tp", shift(-1))
    far = jnp.concatenate([r_m[rows:], r_p[rows:]])
    far_y = jnp.concatenate([c_m, c_p])
    return [own, a_y, a_p, r_p[:rows], far, far_y, a_m, r_m[:rows]], nx


def allreduce(parts, pair_axis, count):
    parts = [p + swap(p, pair_axis) for p in parts]
    bit = 1
    while bit < count:
        perm = tp_perm(count, lambda t, b=bit: t ^ b)
        parts = [p + lax.ppermute(p, "tp", perm) for p in parts]
        bit *= 2
    return parts


def shards(acts, weights, cotangent, start_factors):
    scale = D ** (-0.5)
    count = lax.axis_size("tp")
    weight_part = weights[0]
    grad_out = cotangent[0]
    rows = acts.shape[1]
    blocks, nx = gather_tokens(acts[0], count)
    t = lax.axis_index("tp")
    if nx is None:
        order = jnp.arange(count)
    else:
        k = jnp.arange(count)
        order = ((t // 2 + k // 2) % nx) * 2 + ((t % 2) ^ (k % 2))
    rel = jnp.concatenate(blocks)
    out_rel = jnp.dot(rel, weight_part, preferred_element_type=F32) * scale
    out_rel = out_rel.astype(jnp.bfloat16).reshape(count, rows, -1)
    inverse = jnp.zeros((count,), jnp.int32).at[order].set(jnp.arange(count, dtype=jnp.int32))
    projected = jnp.take(out_rel, inverse, axis=0).reshape(count * rows, -1)[None]
    grad_rel = jnp.take(grad_out.reshape(count, rows, -1), order, axis=0).reshape(count * rows, -1)
    grad = lax.dot_general(rel, grad_rel, (((0,), (0,)), ((), ())), preferred_element_type=F32)
    current = weight_part.astype(F32) - 0.5 * scale * grad
    side = lax.dot_general(current, start_factors, (((0,), (0,)), ((), ())), precision=HIGH)
    backs, orthos = [], []
    eye = jnp.eye(start_factors.shape[1], dtype=F32)
    for step in range(STEPS):
        axis = f"b{step}"
        diff = side - swap(side, axis)
        gram = jnp.dot(diff.T, diff, precision=HIGH)
        mixed = lax.dot_general(diff, current, (((0,), (1,)), ((), ())), precision=HIGH)
        for back_t, ortho_t in zip(backs, orthos):
            inner = jnp.dot(ortho_t, diff, precision=HIGH)
            mixed = mixed - 0.5 * lax.dot_general(inner, back_t, (((0,), (0,)), ((), ())), precision=HIGH)
        gram, mixed = allreduce([gram, mixed], axis, count)
        lower = jnp.linalg.cholesky(0.5 * gram)
        inv = jax.scipy.linalg.solve_triangular(lower, eye, lower=True)
        back_t = jnp.dot(inv, mixed, precision=HIGH)
        ortho_t = jnp.dot(inv, diff.T, precision=HIGH)
        backs.append(back_t)
        orthos.append(ortho_t)
        if step + 1 < STEPS:
            proj = jnp.dot(back_t, start_factors, precision=HIGH)
            side = side - 0.5 * lax.dot_general(ortho_t, proj, (((0,), (0,)), ((), ())), precision=HIGH)
    back_all = jnp.concatenate(backs)
    ortho_all = jnp.concatenate(orthos)
    update = lax.dot_general(back_all, ortho_all, (((0,), (0,)), ((), ())), precision=HIGH)
    new = current - 0.5 * update
    return (projected, new.astype(jnp.bfloat16)[None])


def solution(mesh):
    reps = mesh.shape["rep"]
    high = reps >> STEPS
    names = ("rh",) + tuple(f"b{s}" for s in reversed(range(STEPS)))
    devices = np.asarray(mesh.devices).reshape((high,) + (2,) * STEPS + (mesh.shape["tp"],))
    split = Mesh(devices, names + ("tp",))
    rep = names
    in_specs = (P(rep, "tp", None), P(rep, None, "tp"), P(rep, None, "tp"), P())
    out_specs = (P(rep, None, "tp"), P(rep, None, "tp"))
    return jax.shard_map(shards, mesh=split, in_specs=in_specs, out_specs=out_specs, check_vma=False)
```

time: 689 us -> 316 us (0.46)
  waiting for transfers between devices: 433 us -> 166 us
  blocking collectives: 98.9 us -> 0 us
  matrix products: 101 us -> 63.4 us
  starting transfers between devices: 5.26 us -> 42.3 us
  between operations: 14.2 us -> 1.45 us
  other arithmetic: 20.1 us -> 27.3 us
    psum x3 -> x0, waiting for transfers between devices: 236 us -> none  [shards(): summed = lax.psum(local, 'tp')]
    all_gather x1 -> x0, waiting for transfers between devices: 175 us -> none  [shards(): lax.all_gather(acts, 'tp', axis=1, tiled=True)[0]]
    ppermute x6 -> x34, waiting for transfers between devices: 21 us -> 166 us  [the longest x18 63.1 us: allreduce(): parts = [p + lax.ppermute(p, 'tp', perm) for p in parts]]
    psum x3 -> x0, blocking collectives: 98.9 us -> none  [shards(): gram = lax.psum(jnp.dot(diff.T, diff, precision=HIGH), 'tp')]
    ppermute x6 -> x34, starting transfers between devices: 5.1 us -> 42.3 us  [the longest x18 25.4 us: allreduce(): parts = [p + lax.ppermute(p, 'tp', perm) for p in parts]]
    dot_general x11 -> x25, matrix products: 84.6 us -> 57.6 us  [the longest x3 27.7 us: shards(): lax.dot_general(diff, current, (((0,), (1,)), ((), ())), precision=HIGH)]
    dot_general x3 -> x1, matrix products: 15.2 us -> 5.08 us  [shards(): lax.dot_general(current, start_factors, (((0,), (0,)), ((), ())), precisi...]
  transfers between devices with their start and end apart: 10 -> 34, of which waited for: 9 -> 25; matrix products, arithmetic and copies ran while one was open for 1% -> 13% of each run, Pallas kernels for 0% -> 0%
where the time goes in v1:
time: 316 us; the launch traced here: 310 us
  waiting for transfers between devices  166 us (53%)
  matrix products  63.4 us (20%)
  starting transfers between devices  42.3 us (13%)
  other arithmetic  27.3 us (9%)
  local copies, waits for them, and re-layouts  9.92 us (3%)
    ppermute x18, waiting for transfers between devices, allreduce(): parts = [p + lax.ppermute(p, 'tp', perm) for p in parts]  63.1 us
    ppermute x9, waiting for transfers between devices, swap(): return lax.ppermute(block, axis, [(0, 1), (1, 0)])  39.3 us
    ppermute x1, waiting for transfers between devices, gather_tokens(): r_p = lax.ppermute(jnp.concatenate([a_y, a_p[h:]]), 'tp', shift(-1))  30.3 us
    dot_general x3, matrix products, shards(): lax.dot_general(diff, current, (((0,), (1,)), ((), ())), precision=HIGH)  27.7 us
    ppermute x18, starting transfers between devices, allreduce(): parts = [p + lax.ppermute(p, 'tp', perm) for p in parts]  25.4 us
    ppermute x1, waiting for transfers between devices, gather_tokens(): a_m = lax.ppermute(own, 'tp', shift(1))  20.6 us
    another operation x9, other arithmetic, shards(): lower = jnp.linalg.cholesky(0.5 * gram)  10.8 us
    dot_general x1, matrix products, shards(): lax.dot_general(back_all, ortho_all, (((0,), (0,)), ((), ())), precision=...  10.7 us
  transfers between devices with their start and end apart: 34, of which 25 were waited for; matrix products, arithmetic and copies ran while one was open for 13% of the time, Pallas kernels for 0%

profile of v1, /device:TPU:16, one launch (start us, length us, event | category | flops | bytes accessed | tf_op | source)
XLA Modules:
  0.0 310.0 jit_solution(4641444714663005927)
XLA Ops:
  6.6 20.6 %collective-permute-done.3 = bf16[128,4096]{1,0:T(8,128)(2,1)} collective-permute-done((bf16[128,4096]{1,0:T(8,128)(2,1)}, bf16[128,4096]{1,0:T(8,128)(2,1)}, u32[]{:S(2)}, u32[]{:S(2)}) %collective-permute-start.3) | collective-permute-done | bytes 1048608 | tf_op jit(solution)/shard_map/ppermute | solution.py:35
  34.7 30.3 %collective-permute-done.2 = bf16[192,4096]{1,0:T(8,128)(2,1)S(1)} collective-permute-done((bf16[192,4096]{1,0:T(8,128)(2,1)S(1)}, bf16[192,4096]{1,0:T(8,128)(2,1)S(1)}, u32[]{:S(2)}, u32[]{:S(2)}) %collective-permute-start.2) | collective-permute-done | bytes 1572896 | tf_op jit(solution)/shard_map/ppermute | solution.py:38
  65.1 3.8 %collective-permute-done.4 = bf16[192,4096]{1,0:T(8,128)(2,1)S(1)} collective-permute-done((bf16[192,4096]{1,0:T(8,128)(2,1)S(1)}, bf16[192,4096]{1,0:T(8,128)(2,1)S(1)}, u32[]{:S(2)}, u32[]{:S(2)}) %collective-permute-start.4) | collective-permute-done | bytes 1572896 | tf_op jit(solution)/shard_map/ppermute | solution.py:37
  69.2 3.8 %collective-permute-start.6 = (bf16[64,4096]{1,0:T(8,128)(2,1)S(1)}, bf16[64,4096]{1,0:T(8,128)(2,1)S(1)}, u32[]{:S(2)}, u32[]{:S(2)}) collective-permute-start(bf16[64,4096]{1,0:T(8,128)(2,1)S(1)} %get-tuple-element.7), channel_id=1, source_target_pairs={{0,6},{1,7},{2,0},{3,1},{4,2},{5,3},{6,4},{7,5},{8,14},{9,15},{10,... | collective-permute-start | bytes 1572872 | tf_op jit(solution)/shard_map/ppermute | solution.py:40
  73.2 8.5 %collective-permute-done.5 = bf16[64,4096]{1,0:T(8,128)(2,1)S(1)} collective-permute-done((bf16[64,4096]{1,0:T(8,128)(2,1)S(1)}, bf16[64,4096]{1,0:T(8,128)(2,1)S(1)}, u32[]{:S(2)}, u32[]{:S(2)}) %collective-permute-start.5) | collective-permute-done | bytes 524320 | tf_op jit(solution)/shard_map/ppermute | solution.py:39
  83.2 4.7 %multiply_subtract_fusion = f32[4096,512]{1,0:T(8,128)S(1)} fusion(bf16[1024,4096]{1,0:T(8,128)(2,1)S(1)} %slice_dynamic-update-slice_fusion, bf16[1024,512]{1,0:T(8,128)(2,1)S(1)} %bitcast.91, bf16[1,4096,512]{2,1,0:T(8,128)(2,1)S(1)} %copy-done.4), kind=kOutput, calls=%fused_computation.4 | convolution fusion | flops 4301258752 | bytes 22020096 | tf_op jit(solution)/shard_map/dot_general | solution.py:75
  87.9 5.1 %fusion.55 = f32[512,32]{0,1:T(8,128)S(1)} fusion(f32[4096,512]{1,0:T(8,128)S(1)} %multiply_subtract_fusion, f32[4096,32]{0,1:T(8,128)S(1)} %copy-done.2), kind=kOutput, calls=%fused_computation.120 | convolution fusion | flops 805306368 | bytes 8978432 | tf_op jit(solution)/shard_map/dot_general | solution.py:77
  94.5 7.7 %fusion.57 = f32[32,4096]{1,0:T(8,128)S(1)} fusion(f32[512,32]{0,1:T(8,128)S(1)} %sub.44, f32[4096,512]{1,0:T(8,128)S(1)} %multiply_subtract_fusion), kind=kOutput, calls=%fused_computation.122 | convolution fusion | flops 805306368 | bytes 8978432 | tf_op jit(solution)/shard_map/dot_general | solution.py:84
  107.9 10.8 %collective-permute-done.9 = f32[32,32]{0,1:T(8,128)S(1)} collective-permute-done((f32[32,32]{0,1:T(8,128)S(1)}, f32[32,32]{0,1:T(8,128)S(1)}, u32[]{:S(2)}, u32[]{:S(2)}) %collective-permute-start.9) | collective-permute-done | bytes 4128 | tf_op jit(solution)/shard_map/ppermute | solution.py:51
  118.8 3.7 %collective-permute-done.10 = f32[32,32]{0,1:T(8,128)S(1)} collective-permute-done((f32[32,32]{0,1:T(8,128)S(1)}, f32[32,32]{0,1:T(8,128)S(1)}, u32[]{:S(2)}, u32[]{:S(2)}) %collective-permute-start.10) | collective-permute-done | bytes 4128 | tf_op jit(solution)/shard_map/ppermute | solution.py:51
  122.5 3.0 collective-permute-start.11
  128.0 2.9 cholesky.59
  131.6 6.4 %collective-permute-done.14 = f32[32,4096]{1,0:T(8,128)S(1)} collective-permute-done((f32[32,4096]{1,0:T(8,128)S(1)}, f32[32,4096]{1,0:T(8,128)S(1)}, u32[]{:S(2)}, u32[]{:S(2)}) %collective-permute-start.14) | collective-permute-done | bytes 524320 | tf_op jit(solution)/shard_map/ppermute | solution.py:51
  142.0 9.1 %collective-permute-done.15 = f32[32,4096]{1,0:T(8,128)} collective-permute-done((f32[32,4096]{1,0:T(8,128)S(1)}, f32[32,4096]{1,0:T(8,128)}, u32[]{:S(2)}, u32[]{:S(2)}) %collective-permute-start.15) | collective-permute-done | bytes 524320 | tf_op jit(solution)/shard_map/ppermute | solution.py:51
  154.0 5.4 %collective-permute-done.16 = f32[512,32]{0,1:T(8,128)S(1)} collective-permute-done((f32[512,32]{0,1:T(8,128)S(1)}, f32[512,32]{0,1:T(8,128)S(1)}, u32[]{:S(2)}, u32[]{:S(2)}) %collective-permute-start.16) | collective-permute-done | bytes 65568 | tf_op jit(solution)/shard_map/ppermute | solution.py:16
  160.2 9.9 %convolution_subtract_fusion.1 = f32[32,4096]{1,0:T(8,128)S(1)} fusion(f32[32,4096]{1,0:T(8,128)S(1)} %convolution_multiply_fusion.2, f32[512,32]{0,1:T(8,128)S(1)} %sub.46, f32[4096,512]{1,0:T(8,128)} %copy-done.1), kind=kOutput, calls=%fused_computation.11 | convolution fusion | flops 805437440 | bytes 9502720 | tf_op jit(solution)/shard_map/dot_general | solution.py:84
  170.6 13.5 %collective-permute-done.21 = f32[32,4096]{1,0:T(8,128)S(1)} collective-permute-done((f32[32,4096]{1,0:T(8,128)S(1)}, f32[32,4096]{1,0:T(8,128)S(1)}, u32[]{:S(2)}, u32[]{:S(2)}) %collective-permute-start.21) | collective-permute-done | bytes 524320 | tf_op jit(solution)/shard_map/ppermute | solution.py:16
  186.1 6.8 %collective-permute-done.17 = f32[32,32]{0,1:T(8,128)S(1)} collective-permute-done((f32[32,32]{0,1:T(8,128)S(1)}, f32[32,32]{0,1:T(8,128)S(1)}, u32[]{:S(2)}, u32[]{:S(2)}) %collective-permute-start.17) | collective-permute-done | bytes 4128 | tf_op jit(solution)/shard_map/ppermute | solution.py:16
  194.0 2.6 collective-permute-done.18
  202.3 3.5 %collective-permute-done.20 = f32[32,32]{0,1:T(8,128)S(1)} collective-permute-done((f32[32,32]{0,1:T(8,128)S(1)}, f32[32,32]{0,1:T(8,128)S(1)}, u32[]{:S(2)}, u32[]{:S(2)}) %collective-permute-start.20) | collective-permute-done | bytes 4128 | tf_op jit(solution)/shard_map/ppermute | solution.py:51
  205.8 2.9 cholesky.70
  209.4 4.8 %collective-permute-done.23 = f32[32,4096]{1,0:T(8,128)} collective-permute-done((f32[32,4096]{1,0:T(8,128)S(1)}, f32[32,4096]{1,0:T(8,128)}, u32[]{:S(2)}, u32[]{:S(2)}) %collective-permute-start.23) | collective-permute-done | bytes 524320 | tf_op jit(solution)/shard_map/ppermute | solution.py:51
  216.2 3.1 %collective-permute-start.24 = (f32[32,4096]{1,0:T(8,128)}, f32[32,4096]{1,0:T(8,128)S(1)}, u32[]{:S(2)}, u32[]{:S(2)}) collective-permute-start(f32[32,4096]{1,0:T(8,128)} %add.190), channel_id=1, source_target_pairs={{0,4},{1,5},{2,6},{3,7},{4,0},{5,1},{6,2},{7,3},{8,12},{9,13},{10,... | collective-permute-start | bytes 1572872 | tf_op jit(solution)/shard_map/ppermute | solution.py:51
  222.9 4.2 %collective-permute-done.24 = f32[32,4096]{1,0:T(8,128)S(1)} collective-permute-done((f32[32,4096]{1,0:T(8,128)}, f32[32,4096]{1,0:T(8,128)S(1)}, u32[]{:S(2)}, u32[]{:S(2)}) %collective-permute-start.24) | collective-permute-done | bytes 524320 | tf_op jit(solution)/shard_map/ppermute | solution.py:51
  235.9 10.1 %fusion.1 = f32[32,4096]{1,0:T(8,128)S(1)} fusion(f32[32,4096]{1,0:T(8,128)S(1)} %convolution_multiply_fusion, f32[32,4096]{1,0:T(8,128)S(1)} %convolution_multiply_fusion.1, f32[512,32]{0,1:T(8,128)S(1)} %sub.49, f32[4096,512]{1,0:T(8,128)} %copy-done.1), kind=kOutput, calls=%fused_computation.9 | convolution fusion | flops 805568512 | bytes 10027008 | tf_op jit(solution)/shard_map/dot_general | solution.py:84
  248.4 7.0 %collective-permute-done.26 = f32[32,32]{0,1:T(8,128)S(1)} collective-permute-done((f32[32,32]{0,1:T(8,128)S(1)}, f32[32,32]{0,1:T(8,128)S(1)}, u32[]{:S(2)}, u32[]{:S(2)}) %collective-permute-start.26) | collective-permute-done | bytes 4128 | tf_op jit(solution)/shard_map/ppermute | solution.py:16
  262.8 5.5 %multiply_convert_fusion = bf16[1024,512]{1,0:T(8,128)(2,1)} fusion(bf16[1024,4096]{1,0:T(8,128)(2,1)S(1)} %bitcast.97, bf16[1,4096,512]{2,1,0:T(8,128)(2,1)S(1)} %copy-done.5), kind=kOutput, calls=%fused_computation.14 | convolution fusion | flops 4296015872 | bytes 13631488 | tf_op jit(solution)/shard_map/dot_general | solution.py:70
  270.1 4.2 %collective-permute-start.29 = (f32[32,32]{0,1:T(8,128)S(1)}, f32[32,32]{0,1:T(8,128)S(1)}, u32[]{:S(2)}, u32[]{:S(2)}) collective-permute-start(f32[32,32]{0,1:T(8,128)S(1)} %add.194), channel_id=1, source_target_pairs={{0,4},{1,5},{2,6},{3,7},{4,0},{5,1},{6,2},{7,3},{8,12},{9,13},{10,... | collective-permute-start | bytes 12296 | tf_op jit(solution)/shard_map/ppermute | solution.py:51
  277.1 2.9 cholesky.81
  280.7 5.9 %collective-permute-done.32 = f32[32,4096]{1,0:T(8,128)} collective-permute-done((f32[32,4096]{1,0:T(8,128)S(1)}, f32[32,4096]{1,0:T(8,128)}, u32[]{:S(2)}, u32[]{:S(2)}) %collective-permute-start.32) | collective-permute-done | bytes 524320 | tf_op jit(solution)/shard_map/ppermute | solution.py:51
  292.3 6.2 %collective-permute-done.33 = f32[32,4096]{1,0:T(8,128)S(1)} collective-permute-done((f32[32,4096]{1,0:T(8,128)S(1)}, f32[32,4096]{1,0:T(8,128)S(1)}, u32[]{:S(2)}, u32[]{:S(2)}) %collective-permute-start.33) | collective-permute-done | bytes 524320 | tf_op jit(solution)/shard_map/ppermute | solution.py:51
  299.1 10.7 %fusion = bf16[1,4096,512]{2,1,0:T(8,128)(2,1)} fusion(f32[4096,512]{1,0:T(8,128)} %copy-done.1, f32[32,4096]{1,0:T(8,128)S(1)} %fusion.13, f32[32,4096]{1,0:T(8,128)S(1)} %fusion.15, f32[32,4096]{1,0:T(8,128)S(1)} %fusion.17, f32[32,512]{1,0:T(8,128)S(1)} %fusion.67, f32[32,512]{1,0:T(8,128)S(1)} %fusion.62, f32[32,512]{1,0:T(8,128)S(1)} %fusion.58), kind=kOutput, calls=%fused_computation.5 | convolution fusion | flops 2423095296 | bytes 14352384 | tf_op jit(solution)/shard_map/dot_general | solution.py:100
  (151 shorter events, 78.6 us)
Async XLA Ops:
  0.6 26.5 %collective-permute-start.3 = (bf16[128,4096]{1,0:T(8,128)(2,1)}, bf16[128,4096]{1,0:T(8,128)(2,1)}, u32[]{:S(2)}, u32[]{:S(2)}) collective-permute-start(bf16[128,4096]{1,0:T(8,128)(2,1)} %bitcast.93), channel_id=1, source_target_pairs={{0,2},{1,3},{2,4},{3,5},{4,6},{5,7},{6,0},{7,1},{8,10},{9,11},{10,... | collective-permute-start | bytes 3145736 | tf_op jit(solution)/shard_map/ppermute | solution.py:35
  2.2 26.0 %collective-permute-start.1 = (bf16[128,4096]{1,0:T(8,128)(2,1)}, bf16[128,4096]{1,0:T(8,128)(2,1)}, u32[]{:S(2)}, u32[]{:S(2)}) collective-permute-start(bf16[128,4096]{1,0:T(8,128)(2,1)} %bitcast.94), channel_id=1, source_target_pairs={{0,6},{1,7},{2,0},{3,1},{4,2},{5,3},{6,4},{7,5},{8,14},{9,15},{10,... | collective-permute-start | bytes 3145736 | tf_op jit(solution)/shard_map/ppermute | solution.py:36
  4.0 25.4 %collective-permute-start = (bf16[128,4096]{1,0:T(8,128)(2,1)}, bf16[128,4096]{1,0:T(8,128)(2,1)S(1)}, u32[]{:S(2)}, u32[]{:S(2)}) collective-permute-start(bf16[128,4096]{1,0:T(8,128)(2,1)} %bitcast.95), channel_id=1, source_target_pairs={{0,1},{1,0},{2,3},{3,2},{4,5},{5,4},{6,7},{7,6},{8,9},{9,8},{10,11... | collective-permute-start | bytes 3145736 | tf_op jit(solution)/shard_map/ppermute | solution.py:34
  29.7 35.4 %collective-permute-start.2 = (bf16[192,4096]{1,0:T(8,128)(2,1)S(1)}, bf16[192,4096]{1,0:T(8,128)(2,1)S(1)}, u32[]{:S(2)}, u32[]{:S(2)}) collective-permute-start(bf16[192,4096]{1,0:T(8,128)(2,1)S(1)} %get-tuple-element.12), channel_id=1, source_target_pairs={{0,6},{1,7},{2,0},{3,1},{4,2},{5,3},{6,4},{7,5},{8,14},{9,15},{10,... | collective-permute-start | bytes 4718600 | tf_op jit(solution)/shard_map/ppermute | solution.py:38
  32.9 36.0 %collective-permute-start.4 = (bf16[192,4096]{1,0:T(8,128)(2,1)S(1)}, bf16[192,4096]{1,0:T(8,128)(2,1)S(1)}, u32[]{:S(2)}, u32[]{:S(2)}) collective-permute-start(bf16[192,4096]{1,0:T(8,128)(2,1)S(1)} %get-tuple-element.11), channel_id=1, source_target_pairs={{0,2},{1,3},{2,4},{3,5},{4,6},{5,7},{6,0},{7,1},{8,10},{9,11},{10,... | collective-permute-start | bytes 4718600 | tf_op jit(solution)/shard_map/ppermute | solution.py:37
  69.0 12.7 %collective-permute-start.5 = (bf16[64,4096]{1,0:T(8,128)(2,1)S(1)}, bf16[64,4096]{1,0:T(8,128)(2,1)S(1)}, u32[]{:S(2)}, u32[]{:S(2)}) collective-permute-start(bf16[64,4096]{1,0:T(8,128)(2,1)S(1)} %get-tuple-element.9), channel_id=1, source_target_pairs={{0,2},{1,3},{2,4},{3,5},{4,6},{5,7},{6,0},{7,1},{8,10},{9,11},{10,... | collective-permute-start | bytes 1572872 | tf_op jit(solution)/shard_map/ppermute | solution.py:39
  69.2 12.6 %collective-permute-start.6 = (bf16[64,4096]{1,0:T(8,128)(2,1)S(1)}, bf16[64,4096]{1,0:T(8,128)(2,1)S(1)}, u32[]{:S(2)}, u32[]{:S(2)}) collective-permute-start(bf16[64,4096]{1,0:T(8,128)(2,1)S(1)} %get-tuple-element.7), channel_id=1, source_target_pairs={{0,6},{1,7},{2,0},{3,1},{4,2},{5,3},{6,4},{7,5},{8,14},{9,15},{10,... | collective-permute-start | bytes 1572872 | tf_op jit(solution)/shard_map/ppermute | solution.py:40
  102.3 2.0 collective-permute-start.12
  104.3 21.2 %collective-permute-start.13 = (f32[32,4096]{1,0:T(8,128)S(1)}, f32[32,4096]{1,0:T(8,128)S(1)}, u32[]{:S(2)}, u32[]{:S(2)}) collective-permute-start(f32[32,4096]{1,0:T(8,128)S(1)} %add.180), channel_id=1, source_target_pairs={{0,1},{1,0},{2,3},{3,2},{4,5},{5,4},{6,7},{7,6},{8,9},{9,8},{10,11... | collective-permute-start | bytes 1572872 | tf_op jit(solution)/shard_map/ppermute | solution.py:51
  107.2 11.6 %collective-permute-start.9 = (f32[32,32]{0,1:T(8,128)S(1)}, f32[32,32]{0,1:T(8,128)S(1)}, u32[]{:S(2)}, u32[]{:S(2)}) collective-permute-start(f32[32,32]{0,1:T(8,128)S(1)} %add.176), channel_id=1, source_target_pairs={{0,1},{1,0},{2,3},{3,2},{4,5},{5,4},{6,7},{7,6},{8,9},{9,8},{10,11... | collective-permute-start | bytes 12296 | tf_op jit(solution)/shard_map/ppermute | solution.py:51
  118.7 3.7 %collective-permute-start.10 = (f32[32,32]{0,1:T(8,128)S(1)}, f32[32,32]{0,1:T(8,128)S(1)}, u32[]{:S(2)}, u32[]{:S(2)}) collective-permute-start(f32[32,32]{0,1:T(8,128)S(1)} %add.177), channel_id=1, source_target_pairs={{0,2},{1,3},{2,0},{3,1},{4,6},{5,7},{6,4},{7,5},{8,10},{9,11},{10,... | collective-permute-start | bytes 12296 | tf_op jit(solution)/shard_map/ppermute | solution.py:51
  122.5 5.4 %collective-permute-start.11 = (f32[32,32]{0,1:T(8,128)S(1)}, f32[32,32]{0,1:T(8,128)S(1)}, u32[]{:S(2)}, u32[]{:S(2)}) collective-permute-start(f32[32,32]{0,1:T(8,128)S(1)} %add.178), channel_id=1, source_target_pairs={{0,4},{1,5},{2,6},{3,7},{4,0},{5,1},{6,2},{7,3},{8,12},{9,13},{10,... | collective-permute-start | bytes 12296 | tf_op jit(solution)/shard_map/ppermute | solution.py:51
  125.6 12.4 %collective-permute-start.14 = (f32[32,4096]{1,0:T(8,128)S(1)}, f32[32,4096]{1,0:T(8,128)S(1)}, u32[]{:S(2)}, u32[]{:S(2)}) collective-permute-start(f32[32,4096]{1,0:T(8,128)S(1)} %add.181), channel_id=1, source_target_pairs={{0,2},{1,3},{2,0},{3,1},{4,6},{5,7},{6,4},{7,5},{8,10},{9,11},{10,... | collective-permute-start | bytes 1572872 | tf_op jit(solution)/shard_map/ppermute | solution.py:51
  138.1 13.0 %collective-permute-start.15 = (f32[32,4096]{1,0:T(8,128)S(1)}, f32[32,4096]{1,0:T(8,128)}, u32[]{:S(2)}, u32[]{:S(2)}) collective-permute-start(f32[32,4096]{1,0:T(8,128)S(1)} %add.182), channel_id=1, source_target_pairs={{0,4},{1,5},{2,6},{3,7},{4,0},{5,1},{6,2},{7,3},{8,12},{9,13},{10,... | collective-permute-start | bytes 1572872 | tf_op jit(solution)/shard_map/ppermute | solution.py:51
  153.5 5.9 %collective-permute-start.16 = (f32[512,32]{0,1:T(8,128)S(1)}, f32[512,32]{0,1:T(8,128)S(1)}, u32[]{:S(2)}, u32[]{:S(2)}) collective-permute-start(f32[512,32]{0,1:T(8,128)S(1)} %fusion.12), channel_id=1, source_target_pairs={{0,16},{16,0},{1,17},{17,1},{2,18},{18,2},{3,19},{19,3},{4,20},{20... | collective-permute-start | bytes 196616 | tf_op jit(solution)/shard_map/ppermute | solution.py:16
  170.2 14.0 %collective-permute-start.21 = (f32[32,4096]{1,0:T(8,128)S(1)}, f32[32,4096]{1,0:T(8,128)S(1)}, u32[]{:S(2)}, u32[]{:S(2)}) collective-permute-start(f32[32,4096]{1,0:T(8,128)S(1)} %convolution_subtract_fusion.1), channel_id=1, source_target_pairs={{0,16},{16,0},{1,17},{17,1},{2,18},{18,2},{3,19},{19,3},{4,20},{20... | collective-permute-start | bytes 1572872 | tf_op jit(solution)/shard_map/ppermute | solution.py:16
  184.2 17.4 %collective-permute-start.22 = (f32[32,4096]{1,0:T(8,128)S(1)}, f32[32,4096]{1,0:T(8,128)S(1)}, u32[]{:S(2)}, u32[]{:S(2)}) collective-permute-start(f32[32,4096]{1,0:T(8,128)S(1)} %add.188), channel_id=1, source_target_pairs={{0,1},{1,0},{2,3},{3,2},{4,5},{5,4},{6,7},{7,6},{8,9},{9,8},{10,11... | collective-permute-start | bytes 1572872 | tf_op jit(solution)/shard_map/ppermute | solution.py:51
  186.0 6.9 %collective-permute-start.17 = (f32[32,32]{0,1:T(8,128)S(1)}, f32[32,32]{0,1:T(8,128)S(1)}, u32[]{:S(2)}, u32[]{:S(2)}) collective-permute-start(f32[32,32]{0,1:T(8,128)S(1)} %fusion.60), channel_id=1, source_target_pairs={{0,16},{16,0},{1,17},{17,1},{2,18},{18,2},{3,19},{19,3},{4,20},{20... | collective-permute-start | bytes 12296 | tf_op jit(solution)/shard_map/ppermute | solution.py:16
  192.9 3.7 %collective-permute-start.18 = (f32[32,32]{0,1:T(8,128)S(1)}, f32[32,32]{0,1:T(8,128)S(1)}, u32[]{:S(2)}, u32[]{:S(2)}) collective-permute-start(f32[32,32]{0,1:T(8,128)S(1)} %add.184), channel_id=1, source_target_pairs={{0,1},{1,0},{2,3},{3,2},{4,5},{5,4},{6,7},{7,6},{8,9},{9,8},{10,11... | collective-permute-start | bytes 12296 | tf_op jit(solution)/shard_map/ppermute | solution.py:51
  196.6 3.9 %collective-permute-start.19 = (f32[32,32]{0,1:T(8,128)S(1)}, f32[32,32]{0,1:T(8,128)S(1)}, u32[]{:S(2)}, u32[]{:S(2)}) collective-permute-start(f32[32,32]{0,1:T(8,128)S(1)} %add.185), channel_id=1, source_target_pairs={{0,2},{1,3},{2,0},{3,1},{4,6},{5,7},{6,4},{7,5},{8,10},{9,11},{10,... | collective-permute-start | bytes 12296 | tf_op jit(solution)/shard_map/ppermute | solution.py:51
  200.5 5.2 %collective-permute-start.20 = (f32[32,32]{0,1:T(8,128)S(1)}, f32[32,32]{0,1:T(8,128)S(1)}, u32[]{:S(2)}, u32[]{:S(2)}) collective-permute-start(f32[32,32]{0,1:T(8,128)S(1)} %add.186), channel_id=1, source_target_pairs={{0,4},{1,5},{2,6},{3,7},{4,0},{5,1},{6,2},{7,3},{8,12},{9,13},{10,... | collective-permute-start | bytes 12296 | tf_op jit(solution)/shard_map/ppermute | solution.py:51
  201.7 12.6 %collective-permute-start.23 = (f32[32,4096]{1,0:T(8,128)S(1)}, f32[32,4096]{1,0:T(8,128)}, u32[]{:S(2)}, u32[]{:S(2)}) collective-permute-start(f32[32,4096]{1,0:T(8,128)S(1)} %add.189), channel_id=1, source_target_pairs={{0,2},{1,3},{2,0},{3,1},{4,6},{5,7},{6,4},{7,5},{8,10},{9,11},{10,... | collective-permute-start | bytes 1572872 | tf_op jit(solution)/shard_map/ppermute | solution.py:51
  216.2 10.9 %collective-permute-start.24 = (f32[32,4096]{1,0:T(8,128)}, f32[32,4096]{1,0:T(8,128)S(1)}, u32[]{:S(2)}, u32[]{:S(2)}) collective-permute-start(f32[32,4096]{1,0:T(8,128)} %add.190), channel_id=1, source_target_pairs={{0,4},{1,5},{2,6},{3,7},{4,0},{5,1},{6,2},{7,3},{8,12},{9,13},{10,... | collective-permute-start | bytes 1572872 | tf_op jit(solution)/shard_map/ppermute | solution.py:51
  229.5 4.8 %collective-permute-start.25 = (f32[512,32]{0,1:T(8,128)S(1)}, f32[512,32]{0,1:T(8,128)S(1)}, u32[]{:S(2)}, u32[]{:S(2)}) collective-permute-start(f32[512,32]{0,1:T(8,128)S(1)} %fusion.11), channel_id=1, source_target_pairs={{0,32},{32,0},{1,33},{33,1},{2,34},{34,2},{3,35},{35,3},{4,36},{36... | collective-permute-start | bytes 196616 | tf_op jit(solution)/shard_map/ppermute | solution.py:16
  246.0 14.8 %collective-permute-start.30 = (f32[32,4096]{1,0:T(8,128)S(1)}, f32[32,4096]{1,0:T(8,128)S(1)}, u32[]{:S(2)}, u32[]{:S(2)}) collective-permute-start(f32[32,4096]{1,0:T(8,128)S(1)} %fusion.1), channel_id=1, source_target_pairs={{0,32},{32,0},{1,33},{33,1},{2,34},{34,2},{3,35},{35,3},{4,36},{36... | collective-permute-start | bytes 1572872 | tf_op jit(solution)/shard_map/ppermute | solution.py:16
  248.2 7.2 %collective-permute-start.26 = (f32[32,32]{0,1:T(8,128)S(1)}, f32[32,32]{0,1:T(8,128)S(1)}, u32[]{:S(2)}, u32[]{:S(2)}) collective-permute-start(f32[32,32]{0,1:T(8,128)S(1)} %fusion.64), channel_id=1, source_target_pairs={{0,32},{32,0},{1,33},{33,1},{2,34},{34,2},{3,35},{35,3},{4,36},{36... | collective-permute-start | bytes 12296 | tf_op jit(solution)/shard_map/ppermute | solution.py:16
  255.5 3.7 %collective-permute-start.27 = (f32[32,32]{0,1:T(8,128)S(1)}, f32[32,32]{0,1:T(8,128)S(1)}, u32[]{:S(2)}, u32[]{:S(2)}) collective-permute-start(f32[32,32]{0,1:T(8,128)S(1)} %add.192), channel_id=1, source_target_pairs={{0,1},{1,0},{2,3},{3,2},{4,5},{5,4},{6,7},{7,6},{8,9},{9,8},{10,11... | collective-permute-start | bytes 12296 | tf_op jit(solution)/shard_map/ppermute | solution.py:51
  259.2 10.9 %collective-permute-start.28 = (f32[32,32]{0,1:T(8,128)S(1)}, f32[32,32]{0,1:T(8,128)S(1)}, u32[]{:S(2)}, u32[]{:S(2)}) collective-permute-start(f32[32,32]{0,1:T(8,128)S(1)} %add.193), channel_id=1, source_target_pairs={{0,2},{1,3},{2,0},{3,1},{4,6},{5,7},{6,4},{7,5},{8,10},{9,11},{10,... | collective-permute-start | bytes 12296 | tf_op jit(solution)/shard_map/ppermute | solution.py:51
  261.7 13.8 %collective-permute-start.31 = (f32[32,4096]{1,0:T(8,128)}, f32[32,4096]{1,0:T(8,128)}, u32[]{:S(2)}, u32[]{:S(2)}) collective-permute-start(f32[32,4096]{1,0:T(8,128)} %add.196), channel_id=1, source_target_pairs={{0,1},{1,0},{2,3},{3,2},{4,5},{5,4},{6,7},{7,6},{8,9},{9,8},{10,11... | collective-permute-start | bytes 1572872 | tf_op jit(solution)/shard_map/ppermute | solution.py:51
  270.1 6.9 %collective-permute-start.29 = (f32[32,32]{0,1:T(8,128)S(1)}, f32[32,32]{0,1:T(8,128)S(1)}, u32[]{:S(2)}, u32[]{:S(2)}) collective-permute-start(f32[32,32]{0,1:T(8,128)S(1)} %add.194), channel_id=1, source_target_pairs={{0,4},{1,5},{2,6},{3,7},{4,0},{5,1},{6,2},{7,3},{8,12},{9,13},{10,... | collective-permute-start | bytes 12296 | tf_op jit(solution)/shard_map/ppermute | solution.py:51
  276.7 9.9 %collective-permute-start.32 = (f32[32,4096]{1,0:T(8,128)S(1)}, f32[32,4096]{1,0:T(8,128)}, u32[]{:S(2)}, u32[]{:S(2)}) collective-permute-start(f32[32,4096]{1,0:T(8,128)S(1)} %add.197), channel_id=1, source_target_pairs={{0,2},{1,3},{2,0},{3,1},{4,6},{5,7},{6,4},{7,5},{8,10},{9,11},{10,... | collective-permute-start | bytes 1572872 | tf_op jit(solution)/shard_map/ppermute | solution.py:51
  287.7 10.8 %collective-permute-start.33 = (f32[32,4096]{1,0:T(8,128)S(1)}, f32[32,4096]{1,0:T(8,128)S(1)}, u32[]{:S(2)}, u32[]{:S(2)}) collective-permute-start(f32[32,4096]{1,0:T(8,128)S(1)} %add.198), channel_id=1, source_target_pairs={{0,4},{1,5},{2,6},{3,7},{4,0},{5,1},{6,2},{7,3},{8,12},{9,13},{10,... | collective-permute-start | bytes 1572872 | tf_op jit(solution)/shard_map/ppermute | solution.py:51
  (10 other events, 188.4 us)

commit v2 on v1

--- a/solution.py
+++ b/solution.py
@@ -9,6 +9,7 @@
 
 
 HIGH = lax.Precision.HIGHEST
+FAST = lax.Precision.HIGH
 F32 = jnp.float32
 
 
@@ -29,18 +30,17 @@
     def shift(d):
         return tp_perm(count, lambda t: ((t // 2 + d) % nx) * 2 + t % 2)
 
-    rows = own.shape[0]
-    h = rows // 2
-    a_y = lax.ppermute(own, "tp", tp_perm(count, lambda t: t ^ 1))
+    h = own.shape[0] // 2
+    pair = tp_perm(count, lambda t: t ^ 1)
+    a_y = lax.ppermute(own, "tp", pair)
     a_m = lax.ppermute(own, "tp", shift(1))
     a_p = lax.ppermute(own, "tp", shift(-1))
-    r_m = lax.ppermute(jnp.concatenate([a_y, a_m[:h]]), "tp", shift(1))
-    r_p = lax.ppermute(jnp.concatenate([a_y, a_p[h:]]), "tp", shift(-1))
-    c_m = lax.ppermute(r_m[:h], "tp", shift(1))
-    c_p = lax.ppermute(r_p[h:rows], "tp", shift(-1))
-    far = jnp.concatenate([r_m[rows:], r_p[rows:]])
-    far_y = jnp.concatenate([c_m, c_p])
-    return [own, a_y, a_p, r_p[:rows], far, far_y, a_m, r_m[:rows]], nx
+    b_m = lax.ppermute(a_y, "tp", shift(1))
+    b_p = lax.ppermute(a_p, "tp", shift(-1))
+    b_y = lax.ppermute(a_p, "tp", pair)
+    c_y = lax.ppermute(b_p[:h], "tp", pair)
+    c_p = lax.ppermute(b_y[h:], "tp", shift(-1))
+    return [own, a_y, a_p, b_y, b_p, jnp.concatenate([c_y, c_p]), a_m, b_m], nx
 
 
 def allreduce(parts, pair_axis, count):
@@ -74,18 +74,21 @@
     grad_rel = jnp.take(grad_out.reshape(count, rows, -1), order, axis=0).reshape(count * rows, -1)
     grad = lax.dot_general(rel, grad_rel, (((0,), (0,)), ((), ())), preferred_element_type=F32)
     current = weight_part.astype(F32) - 0.5 * scale * grad
-    side = lax.dot_general(current, start_factors, (((0,), (0,)), ((), ())), precision=HIGH)
+    side = lax.dot_general(current, start_factors, (((0,), (0,)), ((), ())), precision=FAST)
     backs, orthos = [], []
     eye = jnp.eye(start_factors.shape[1], dtype=F32)
     for step in range(STEPS):
         axis = f"b{step}"
         diff = side - swap(side, axis)
         gram = jnp.dot(diff.T, diff, precision=HIGH)
-        mixed = lax.dot_general(diff, current, (((0,), (1,)), ((), ())), precision=HIGH)
+        mixed = lax.dot_general(diff, current, (((0,), (1,)), ((), ())), precision=FAST)
         for back_t, ortho_t in zip(backs, orthos):
             inner = jnp.dot(ortho_t, diff, precision=HIGH)
             mixed = mixed - 0.5 * lax.dot_general(inner, back_t, (((0,), (0,)), ((), ())), precision=HIGH)
-        gram, mixed = allreduce([gram, mixed], axis, count)
+        width = mixed.shape[0]
+        packed = jnp.concatenate([jnp.pad(gram, ((0, 0), (0, 128 - width))), mixed], axis=1)
+        (packed,) = allreduce([packed], axis, count)
+        gram, mixed = packed[:, :width], packed[:, 128:]
         lower = jnp.linalg.cholesky(0.5 * gram)
         inv = jax.scipy.linalg.solve_triangular(lower, eye, lower=True)
         back_t = jnp.dot(inv, mixed, precision=HIGH)
@@ -97,7 +100,7 @@
             side = side - 0.5 * lax.dot_general(ortho_t, proj, (((0,), (0,)), ((), ())), precision=HIGH)
     back_all = jnp.concatenate(backs)
     ortho_all = jnp.concatenate(orthos)
-    update = lax.dot_general(back_all, ortho_all, (((0,), (0,)), ((), ())), precision=HIGH)
+    update = lax.dot_general(back_all, ortho_all, (((0,), (0,)), ((), ())), precision=FAST)
     new = current - 0.5 * update
     return (projected, new.astype(jnp.bfloat16)[None])
 

time: 316 us -> 357 us (1.13)
  local copies, waits for them, and re-layouts: 9.92 us -> 48.3 us
  other arithmetic: 27.3 us -> 45.6 us
  starting transfers between devices: 42.3 us -> 35.2 us
  waiting for transfers between devices: 166 us -> 160 us
    ppermute x1, waiting for transfers between devices: 20.6 us -> 0.01 us  [gather_tokens(): a_m = lax.ppermute(own, 'tp', shift(1))]
    ppermute x0 -> x9, local copies, waits for them, and re-layouts: none -> 20.4 us  [allreduce(): parts = [p + lax.ppermute(p, 'tp', perm) for p in parts]]
    ppermute x1, waiting for transfers between devices: 0.01 us -> 19.8 us  [gather_tokens(): a_p = lax.ppermute(own, 'tp', shift(-1))]
    add x12 -> x9, other arithmetic: 4.45 us -> 21.7 us  [allreduce(): parts = [p + lax.ppermute(p, 'tp', perm) for p in parts]]
    ppermute x18 -> x9, waiting for transfers between devices: 63.1 us -> 80.2 us  [allreduce(): parts = [p + lax.ppermute(p, 'tp', perm) for p in parts]]
    add x0 -> x9, local copies, waits for them, and re-layouts: none -> 16.1 us  [the longest x6 10.1 us: allreduce(): parts = [p + lax.ppermute(p, 'tp', perm) for p in parts]]
    ppermute x5 -> x6, waiting for transfers between devices: 42.7 us -> 28 us  [the longest x1 19.5 us: gather_tokens(): b_p = lax.ppermute(a_p, 'tp', shift(-1))]
    ppermute x18 -> x9, starting transfers between devices: 25.4 us -> 15 us  [allreduce(): parts = [p + lax.ppermute(p, 'tp', perm) for p in parts]]
  transfers between devices with their start and end apart: 34 -> 23, of which waited for: 25 -> 18; matrix products, arithmetic and copies ran while one was open for 13% -> 7% of each run, Pallas kernels for 0% -> 0%
where the time goes in v2:
time: 357 us; the launch traced here: 352 us
  waiting for transfers between devices  160 us (45%)
  matrix products  61.2 us (17%)
  local copies, waits for them, and re-layouts  48.3 us (14%)
  other arithmetic  45.6 us (13%)
  starting transfers between devices  35.2 us (10%)
    ppermute x9, waiting for transfers between devices, allreduce(): parts = [p + lax.ppermute(p, 'tp', perm) for p in parts]  80.2 us
    ppermute x6, waiting for transfers between devices, swap(): return lax.ppermute(block, axis, [(0, 1), (1, 0)])  32.2 us
    add x9, other arithmetic, allreduce(): parts = [p + lax.ppermute(p, 'tp', perm) for p in parts]  21.7 us
    ppermute x9, local copies, waits for them, and re-layouts, allreduce(): parts = [p + lax.ppermute(p, 'tp', perm) for p in parts]  20.4 us
    ppermute x1, waiting for transfers between devices, gather_tokens(): a_p = lax.ppermute(own, 'tp', shift(-1))  19.8 us
    ppermute x1, waiting for transfers between devices, gather_tokens(): b_p = lax.ppermute(a_p, 'tp', shift(-1))  19.5 us
    dot_general x3, matrix products, shards(): lax.dot_general(diff, current, (((0,), (1,)), ((), ())), precision=FAST)  18 us
    ppermute x9, starting transfers between devices, allreduce(): parts = [p + lax.ppermute(p, 'tp', perm) for p in parts]  15 us
  transfers between devices with their start and end apart: 23, of which 18 were waited for; matrix products, arithmetic and copies ran while one was open for 7% of the time, Pallas kernels for 0%

profile of v2, /device:TPU:16, one launch (start us, length us, event | category | flops | bytes accessed | tf_op | source)
XLA Modules:
  0.0 352.0 jit_solution(14648589993044015128)
XLA Ops:
  7.4 19.8 %collective-permute-done.1 = bf16[128,4096]{1,0:T(8,128)(2,1)} collective-permute-done((bf16[128,4096]{1,0:T(8,128)(2,1)}, bf16[128,4096]{1,0:T(8,128)(2,1)}, u32[]{:S(2)}, u32[]{:S(2)}) %collective-permute-start.1) | collective-permute-done | bytes 1048608 | tf_op jit(solution)/shard_map/ppermute | solution.py:37
  28.0 3.7 %collective-permute-start.3 = (bf16[128,4096]{1,0:T(8,128)(2,1)}, bf16[128,4096]{1,0:T(8,128)(2,1)S(1)}, u32[]{:S(2)}, u32[]{:S(2)}) collective-permute-start(bf16[128,4096]{1,0:T(8,128)(2,1)} %collective-permute-done.1), channel_id=1, source_target_pairs={{0,6},{1,7},{2,0},{3,1},{4,2},{5,3},{6,4},{7,5},{8,14},{9,15},{10,... | collective-permute-start | bytes 3145736 | tf_op jit(solution)/shard_map/ppermute | solution.py:39
  33.5 19.5 %collective-permute-done.3 = bf16[128,4096]{1,0:T(8,128)(2,1)S(1)} collective-permute-done((bf16[128,4096]{1,0:T(8,128)(2,1)}, bf16[128,4096]{1,0:T(8,128)(2,1)S(1)}, u32[]{:S(2)}, u32[]{:S(2)}) %collective-permute-start.3) | collective-permute-done | bytes 1048608 | tf_op jit(solution)/shard_map/ppermute | solution.py:39
  54.4 4.2 %collective-permute-start.5 = (bf16[64,4096]{1,0:T(8,128)(2,1)S(1)}, bf16[64,4096]{1,0:T(8,128)(2,1)S(1)}, u32[]{:S(2)}, u32[]{:S(2)}) collective-permute-start(bf16[64,4096]{1,0:T(8,128)(2,1)S(1)} %slice.45), channel_id=1, source_target_pairs={{0,6},{1,7},{2,0},{3,1},{4,2},{5,3},{6,4},{7,5},{8,14},{9,15},{10,... | collective-permute-start | bytes 1572872 | tf_op jit(solution)/shard_map/ppermute | solution.py:42
  58.8 5.7 %collective-permute-done.4 = bf16[64,4096]{1,0:T(8,128)(2,1)S(1)} collective-permute-done((bf16[64,4096]{1,0:T(8,128)(2,1)S(1)}, bf16[64,4096]{1,0:T(8,128)(2,1)S(1)}, u32[]{:S(2)}, u32[]{:S(2)}) %collective-permute-start.4) | collective-permute-done | bytes 524320 | tf_op jit(solution)/shard_map/ppermute | solution.py:41
  68.7 4.7 %multiply_subtract_fusion = f32[4096,512]{1,0:T(8,128)S(1)} fusion(bf16[1024,4096]{1,0:T(8,128)(2,1)S(1)} %constant_dynamic-update-slice_fusion, bf16[1024,512]{1,0:T(8,128)(2,1)S(1)} %bitcast.90, bf16[1,4096,512]{2,1,0:T(8,128)(2,1)S(1)} %copy-done.11), kind=kOutput, calls=%fused_computation.4 | convolution fusion | flops 4301258752 | bytes 22020096 | tf_op jit(solution)/shard_map/dot_general | solution.py:75
  77.4 3.9 %fusion.58 = f32[32,4096]{1,0:T(8,128)S(1)} fusion(f32[512,32]{0,1:T(8,128)S(1)} %sub.44, f32[4096,512]{1,0:T(8,128)S(1)} %multiply_subtract_fusion), kind=kOutput, calls=%fused_computation.124 | convolution fusion | flops 402653184 | bytes 8978432 | tf_op jit(solution)/shard_map/dot_general | solution.py:84
  86.5 11.6 %collective-permute-done.10 = f32[32,4224]{1,0:T(8,128)S(1)} collective-permute-done((f32[32,4224]{1,0:T(8,128)S(1)}, f32[32,4224]{1,0:T(8,128)S(1)}, u32[]{:S(2)}, u32[]{:S(2)}) %collective-permute-start.10) | collective-permute-done | bytes 540704 | tf_op jit(solution)/shard_map/ppermute | solution.py:51
  104.0 13.8 %collective-permute-done.11 = f32[32,4224]{1,0:T(8,128)} collective-permute-done((f32[32,4224]{1,0:T(8,128)}, f32[32,4224]{1,0:T(8,128)}, u32[]{:S(2)}, u32[]{:S(2)}) %collective-permute-start.11) | collective-permute-done | bytes 540704 | tf_op jit(solution)/shard_map/ppermute | solution.py:51
  120.8 3.2 add.148
  126.2 3.5 collective-permute-start.12
  129.7 11.3 %collective-permute-done.12 = f32[32,4224]{1,0:T(8,128)} collective-permute-done((f32[32,4224]{1,0:T(8,128)S(1)}, f32[32,4224]{1,0:T(8,128)}, u32[]{:S(2)}, u32[]{:S(2)}) %collective-permute-start.12) | collective-permute-done | bytes 540704 | tf_op jit(solution)/shard_map/ppermute | solution.py:51
  153.7 3.8 %fusion.8 = f32[32,4096]{1,0:T(8,128)S(1)} fusion(f32[32,32]{1,0:T(8,128)S(1)} %fusion.28, f32[32,4224]{0,1:T(8,128)} %copy-done.5), kind=kOutput, calls=%fused_computation.18 | convolution fusion | flops 50331648 | bytes 2625536 | tf_op jit(solution)/shard_map/dot_general | solution.py:94
  159.0 5.2 %collective-permute-done.13 = f32[512,32]{0,1:T(8,128)S(1)} collective-permute-done((f32[512,32]{0,1:T(8,128)S(1)}, f32[512,32]{0,1:T(8,128)S(1)}, u32[]{:S(2)}, u32[]{:S(2)}) %collective-permute-start.13) | collective-permute-done | bytes 65568 | tf_op jit(solution)/shard_map/ppermute | solution.py:17
  165.2 7.1 %convolution_subtract_fusion.1 = f32[32,4096]{1,0:T(8,128)S(1)} fusion(f32[32,4096]{1,0:T(8,128)S(1)} %convolution_multiply_fusion.2, f32[512,32]{0,1:T(8,128)S(1)} %sub.46, f32[4096,512]{1,0:T(8,128)} %copy-done.2), kind=kOutput, calls=%fused_computation.11 | convolution fusion | flops 402784256 | bytes 9502720 | tf_op jit(solution)/shard_map/dot_general | solution.py:84
  173.0 14.0 %collective-permute-done.14 = f32[32,4224]{1,0:T(8,128)S(1)} collective-permute-done((f32[32,4224]{1,0:T(8,128)S(1)}, f32[32,4224]{1,0:T(8,128)S(1)}, u32[]{:S(2)}, u32[]{:S(2)}) %collective-permute-start.14) | collective-permute-done | bytes 540704 | tf_op jit(solution)/shard_map/ppermute | solution.py:17
  189.4 7.4 %collective-permute-done.15 = f32[32,4224]{1,0:T(8,128)S(1)} collective-permute-done((f32[32,4224]{1,0:T(8,128)S(1)}, f32[32,4224]{1,0:T(8,128)S(1)}, u32[]{:S(2)}, u32[]{:S(2)}) %collective-permute-start.15) | collective-permute-done | bytes 540704 | tf_op jit(solution)/shard_map/ppermute | solution.py:51
  203.5 8.8 %collective-permute-done.16 = f32[32,4224]{1,0:T(8,128)} collective-permute-done((f32[32,4224]{1,0:T(8,128)}, f32[32,4224]{1,0:T(8,128)}, u32[]{:S(2)}, u32[]{:S(2)}) %collective-permute-start.16) | collective-permute-done | bytes 540704 | tf_op jit(solution)/shard_map/ppermute | solution.py:51
  212.3 3.0 copy.55
  215.3 3.2 add.152
  220.7 3.3 collective-permute-start.17
  224.0 7.7 %collective-permute-done.17 = f32[32,4224]{1,0:T(8,128)} collective-permute-done((f32[32,4224]{1,0:T(8,128)S(1)}, f32[32,4224]{1,0:T(8,128)}, u32[]{:S(2)}, u32[]{:S(2)}) %collective-permute-start.17) | collective-permute-done | bytes 540704 | tf_op jit(solution)/shard_map/ppermute | solution.py:51
  244.5 3.8 %fusion.6 = f32[32,4096]{1,0:T(8,128)S(1)} fusion(f32[32,32]{1,0:T(8,128)S(1)} %fusion.26, f32[32,4224]{0,1:T(8,128)} %copy-done.6), kind=kOutput, calls=%fused_computation.16 | convolution fusion | flops 50331648 | bytes 2625536 | tf_op jit(solution)/shard_map/dot_general | solution.py:94
  257.0 7.1 %fusion.1 = f32[32,4096]{1,0:T(8,128)S(1)} fusion(f32[32,4096]{1,0:T(8,128)S(1)} %convolution_multiply_fusion, f32[32,4096]{1,0:T(8,128)S(1)} %convolution_multiply_fusion.1, f32[512,32]{0,1:T(8,128)S(1)} %sub.49, f32[4096,512]{1,0:T(8,128)} %copy-done.2), kind=kOutput, calls=%fused_computation.9 | convolution fusion | flops 402915328 | bytes 10027008 | tf_op jit(solution)/shard_map/dot_general | solution.py:84
  266.0 7.6 %collective-permute-done.19 = f32[32,4224]{1,0:T(8,128)S(1)} collective-permute-done((f32[32,4224]{1,0:T(8,128)S(1)}, f32[32,4224]{1,0:T(8,128)S(1)}, u32[]{:S(2)}, u32[]{:S(2)}) %collective-permute-start.19) | collective-permute-done | bytes 540704 | tf_op jit(solution)/shard_map/ppermute | solution.py:17
  275.7 7.4 %collective-permute-done.20 = f32[32,4224]{1,0:T(8,128)S(1)} collective-permute-done((f32[32,4224]{1,0:T(8,128)S(1)}, f32[32,4224]{1,0:T(8,128)S(1)}, u32[]{:S(2)}, u32[]{:S(2)}) %collective-permute-start.20) | collective-permute-done | bytes 540704 | tf_op jit(solution)/shard_map/ppermute | solution.py:51
  289.9 12.2 %collective-permute-done.21 = f32[32,4224]{1,0:T(8,128)S(1)} collective-permute-done((f32[32,4224]{1,0:T(8,128)}, f32[32,4224]{1,0:T(8,128)S(1)}, u32[]{:S(2)}, u32[]{:S(2)}) %collective-permute-start.21) | collective-permute-done | bytes 540704 | tf_op jit(solution)/shard_map/ppermute | solution.py:51
  308.1 5.2 %collective-permute-start.22 = (f32[32,4224]{1,0:T(8,128)}, f32[32,4224]{1,0:T(8,128)}, u32[]{:S(2)}, u32[]{:S(2)}) collective-permute-start(f32[32,4224]{1,0:T(8,128)} %copy.63), channel_id=1, source_target_pairs={{0,4},{1,5},{2,6},{3,7},{4,0},{5,1},{6,2},{7,3},{8,12},{9,13},{10,... | collective-permute-start | bytes 1622024 | tf_op jit(solution)/shard_map/ppermute | solution.py:51
  313.2 10.0 %multiply_convert_fusion = bf16[1024,512]{1,0:T(8,128)(2,1)} fusion(bf16[1024,4096]{1,0:T(8,128)(2,1)} %copy-done.10, bf16[1,4096,512]{2,1,0:T(8,128)(2,1)} %param.10), kind=kOutput, calls=%fused_computation.20 | convolution fusion | flops 4296015872 | bytes 13631488 | tf_op jit(solution)/shard_map/dot_general | solution.py:70
  326.2 3.0 copy.64
  340.2 3.9 %fusion.4 = f32[32,4096]{1,0:T(8,128)S(1)} fusion(f32[32,32]{1,0:T(8,128)S(1)} %fusion.24, f32[32,4224]{0,1:T(8,128)} %copy-done.7), kind=kOutput, calls=%fused_computation.14 | convolution fusion | flops 50331648 | bytes 2625536 | tf_op jit(solution)/shard_map/dot_general | solution.py:94
  344.2 7.6 %fusion = bf16[1,4096,512]{2,1,0:T(8,128)(2,1)} fusion(f32[4096,512]{1,0:T(8,128)} %copy-done.2, f32[32,4096]{1,0:T(8,128)S(1)} %fusion.4, f32[32,4096]{1,0:T(8,128)} %copy-done.8, f32[32,4096]{1,0:T(8,128)} %copy-done.4, f32[32,512]{1,0:T(8,128)S(1)} %fusion.68, f32[32,512]{1,0:T(8,128)S(1)} %fusion.63, f32[32,512]{1,0:T(8,128)S(1)} %fusion.59), kind=kOutput, calls=%fused_computation.5 | convolution fusion | flops 1215135744 | bytes 14352384 | tf_op jit(solution)/shard_map/dot_general | solution.py:103
  (149 shorter events, 114.7 us)
Async XLA Ops:
  0.6 4.8 %copy-start = (bf16[1,1024,512]{2,1,0:T(8,128)(2,1)S(1)}, bf16[1,1024,512]{2,1,0:T(8,128)(2,1)}, u32[]{:S(2)}) copy-start(bf16[1,1024,512]{2,1,0:T(8,128)(2,1)} %param.11) | copy-start | bytes 3145732
  0.6 31.2 %collective-permute-start = (bf16[128,4096]{1,0:T(8,128)(2,1)}, bf16[128,4096]{1,0:T(8,128)(2,1)S(1)}, u32[]{:S(2)}, u32[]{:S(2)}) collective-permute-start(bf16[128,4096]{1,0:T(8,128)(2,1)} %bitcast.93), channel_id=1, source_target_pairs={{0,1},{1,0},{2,3},{3,2},{4,5},{5,4},{6,7},{7,6},{8,9},{9,8},{10,11... | collective-permute-start | bytes 3145736 | tf_op jit(solution)/shard_map/ppermute | solution.py:35
  2.0 25.2 %collective-permute-start.1 = (bf16[128,4096]{1,0:T(8,128)(2,1)}, bf16[128,4096]{1,0:T(8,128)(2,1)}, u32[]{:S(2)}, u32[]{:S(2)}) collective-permute-start(bf16[128,4096]{1,0:T(8,128)(2,1)} %bitcast.94), channel_id=1, source_target_pairs={{0,6},{1,7},{2,0},{3,1},{4,2},{5,3},{6,4},{7,5},{8,14},{9,15},{10,... | collective-permute-start | bytes 3145736 | tf_op jit(solution)/shard_map/ppermute | solution.py:37
  4.8 62.5 %collective-permute-start.6 = (bf16[128,4096]{1,0:T(8,128)(2,1)}, bf16[128,4096]{1,0:T(8,128)(2,1)}, u32[]{:S(2)}, u32[]{:S(2)}) collective-permute-start(bf16[128,4096]{1,0:T(8,128)(2,1)} %bitcast.95), channel_id=1, source_target_pairs={{0,2},{1,3},{2,4},{3,5},{4,6},{5,7},{6,0},{7,1},{8,10},{9,11},{10,... | collective-permute-start | bytes 3145736 | tf_op jit(solution)/shard_map/ppermute | solution.py:36
  27.2 27.2 %collective-permute-start.2 = (bf16[128,4096]{1,0:T(8,128)(2,1)}, bf16[128,4096]{1,0:T(8,128)(2,1)S(1)}, u32[]{:S(2)}, u32[]{:S(2)}) collective-permute-start(bf16[128,4096]{1,0:T(8,128)(2,1)} %collective-permute-done.1), channel_id=1, source_target_pairs={{0,1},{1,0},{2,3},{3,2},{4,5},{5,4},{6,7},{7,6},{8,9},{9,8},{10,11... | collective-permute-start | bytes 3145736 | tf_op jit(solution)/shard_map/ppermute | solution.py:40
  28.0 25.0 %collective-permute-start.3 = (bf16[128,4096]{1,0:T(8,128)(2,1)}, bf16[128,4096]{1,0:T(8,128)(2,1)S(1)}, u32[]{:S(2)}, u32[]{:S(2)}) collective-permute-start(bf16[128,4096]{1,0:T(8,128)(2,1)} %collective-permute-done.1), channel_id=1, source_target_pairs={{0,6},{1,7},{2,0},{3,1},{4,2},{5,3},{6,4},{7,5},{8,14},{9,15},{10,... | collective-permute-start | bytes 3145736 | tf_op jit(solution)/shard_map/ppermute | solution.py:39
  31.8 36.9 %copy-start.11 = (bf16[1,4096,512]{2,1,0:T(8,128)(2,1)S(1)}, bf16[1,4096,512]{2,1,0:T(8,128)(2,1)}, u32[]{:S(2)}) copy-start(bf16[1,4096,512]{2,1,0:T(8,128)(2,1)} %param.10) | copy-start | bytes 12582916
  31.9 36.8 %collective-permute-start.7 = (bf16[128,4096]{1,0:T(8,128)(2,1)S(1)}, bf16[128,4096]{1,0:T(8,128)(2,1)S(1)}, u32[]{:S(2)}, u32[]{:S(2)}) collective-permute-start(bf16[128,4096]{1,0:T(8,128)(2,1)S(1)} %collective-permute-done), channel_id=1, source_target_pairs={{0,2},{1,3},{2,4},{3,5},{4,6},{5,7},{6,0},{7,1},{8,10},{9,11},{10,... | collective-permute-start | bytes 3145736 | tf_op jit(solution)/shard_map/ppermute | solution.py:38
  53.0 11.5 %collective-permute-start.4 = (bf16[64,4096]{1,0:T(8,128)(2,1)S(1)}, bf16[64,4096]{1,0:T(8,128)(2,1)S(1)}, u32[]{:S(2)}, u32[]{:S(2)}) collective-permute-start(bf16[64,4096]{1,0:T(8,128)(2,1)S(1)} %slice.44), channel_id=1, source_target_pairs={{0,1},{1,0},{2,3},{3,2},{4,5},{5,4},{6,7},{7,6},{8,9},{9,8},{10,11... | collective-permute-start | bytes 1572872 | tf_op jit(solution)/shard_map/ppermute | solution.py:41
  54.4 12.8 %collective-permute-start.5 = (bf16[64,4096]{1,0:T(8,128)(2,1)S(1)}, bf16[64,4096]{1,0:T(8,128)(2,1)S(1)}, u32[]{:S(2)}, u32[]{:S(2)}) collective-permute-start(bf16[64,4096]{1,0:T(8,128)(2,1)S(1)} %slice.45), channel_id=1, source_target_pairs={{0,6},{1,7},{2,0},{3,1},{4,2},{5,3},{6,4},{7,5},{8,14},{9,15},{10,... | collective-permute-start | bytes 1572872 | tf_op jit(solution)/shard_map/ppermute | solution.py:42
  68.7 4.7 %copy-start.10 = (bf16[1024,4096]{1,0:T(8,128)(2,1)}, bf16[1024,4096]{1,0:T(8,128)(2,1)S(1)}, u32[]{:S(2)}) copy-start(bf16[1024,4096]{1,0:T(8,128)(2,1)S(1)} %constant_dynamic-update-slice_fusion) | copy-start | bytes 25165828
  68.7 4.7 %copy-start.9 = (f32[4096,32]{0,1:T(8,128)S(1)}, f32[4096,32]{0,1:T(8,128)}, u32[]{:S(2)}) copy-start(f32[4096,32]{0,1:T(8,128)} %param.12) | copy-start | bytes 1572868
  73.4 7.9 %copy-start.2 = (f32[4096,512]{1,0:T(8,128)}, f32[4096,512]{1,0:T(8,128)S(1)}, u32[]{:S(2)}) copy-start(f32[4096,512]{1,0:T(8,128)S(1)} %multiply_subtract_fusion) | copy-start | bytes 25165828
  75.9 1.3 collective-permute-start.8
  81.4 2.0 collective-permute-start.9
  83.5 14.6 %collective-permute-start.10 = (f32[32,4224]{1,0:T(8,128)S(1)}, f32[32,4224]{1,0:T(8,128)S(1)}, u32[]{:S(2)}, u32[]{:S(2)}) collective-permute-start(f32[32,4224]{1,0:T(8,128)S(1)} %fusion.53), channel_id=1, source_target_pairs={{0,1},{1,0},{2,3},{3,2},{4,5},{5,4},{6,7},{7,6},{8,9},{9,8},{10,11... | collective-permute-start | bytes 1622024 | tf_op jit(solution)/shard_map/ppermute | solution.py:51
  104.0 13.8 %collective-permute-start.11 = (f32[32,4224]{1,0:T(8,128)}, f32[32,4224]{1,0:T(8,128)}, u32[]{:S(2)}, u32[]{:S(2)}) collective-permute-start(f32[32,4224]{1,0:T(8,128)} %copy.47), channel_id=1, source_target_pairs={{0,2},{1,3},{2,0},{3,1},{4,6},{5,7},{6,4},{7,5},{8,10},{9,11},{10,... | collective-permute-start | bytes 1622024 | tf_op jit(solution)/shard_map/ppermute | solution.py:51
  126.2 14.8 %collective-permute-start.12 = (f32[32,4224]{1,0:T(8,128)S(1)}, f32[32,4224]{1,0:T(8,128)}, u32[]{:S(2)}, u32[]{:S(2)}) collective-permute-start(f32[32,4224]{1,0:T(8,128)S(1)} %copy.49), channel_id=1, source_target_pairs={{0,4},{1,5},{2,6},{3,7},{4,0},{5,1},{6,2},{7,3},{8,12},{9,13},{10,... | collective-permute-start | bytes 1622024 | tf_op jit(solution)/shard_map/ppermute | solution.py:51
  157.5 98.9 %copy-start.4 = (f32[32,4096]{1,0:T(8,128)}, f32[32,4096]{1,0:T(8,128)S(1)}, u32[]{:S(2)}) copy-start(f32[32,4096]{1,0:T(8,128)S(1)} %fusion.8) | copy-start | bytes 1572868
  158.3 5.9 %collective-permute-start.13 = (f32[512,32]{0,1:T(8,128)S(1)}, f32[512,32]{0,1:T(8,128)S(1)}, u32[]{:S(2)}, u32[]{:S(2)}) collective-permute-start(f32[512,32]{0,1:T(8,128)S(1)} %fusion.18), channel_id=1, source_target_pairs={{0,16},{16,0},{1,17},{17,1},{2,18},{18,2},{3,19},{19,3},{4,20},{20... | collective-permute-start | bytes 196616 | tf_op jit(solution)/shard_map/ppermute | solution.py:17
  172.3 14.7 %collective-permute-start.14 = (f32[32,4224]{1,0:T(8,128)S(1)}, f32[32,4224]{1,0:T(8,128)S(1)}, u32[]{:S(2)}, u32[]{:S(2)}) collective-permute-start(f32[32,4224]{1,0:T(8,128)S(1)} %select_maximum_fusion.1), channel_id=1, source_target_pairs={{0,16},{16,0},{1,17},{17,1},{2,18},{18,2},{3,19},{19,3},{4,20},{20... | collective-permute-start | bytes 1622024 | tf_op jit(solution)/shard_map/ppermute | solution.py:17
  187.1 9.7 %collective-permute-start.15 = (f32[32,4224]{1,0:T(8,128)S(1)}, f32[32,4224]{1,0:T(8,128)S(1)}, u32[]{:S(2)}, u32[]{:S(2)}) collective-permute-start(f32[32,4224]{1,0:T(8,128)S(1)} %fusion.54), channel_id=1, source_target_pairs={{0,1},{1,0},{2,3},{3,2},{4,5},{5,4},{6,7},{7,6},{8,9},{9,8},{10,11... | collective-permute-start | bytes 1622024 | tf_op jit(solution)/shard_map/ppermute | solution.py:51
  202.6 9.7 %collective-permute-start.16 = (f32[32,4224]{1,0:T(8,128)}, f32[32,4224]{1,0:T(8,128)}, u32[]{:S(2)}, u32[]{:S(2)}) collective-permute-start(f32[32,4224]{1,0:T(8,128)} %copy.54), channel_id=1, source_target_pairs={{0,2},{1,3},{2,0},{3,1},{4,6},{5,7},{6,4},{7,5},{8,10},{9,11},{10,... | collective-permute-start | bytes 1622024 | tf_op jit(solution)/shard_map/ppermute | solution.py:51
  220.7 11.0 %collective-permute-start.17 = (f32[32,4224]{1,0:T(8,128)S(1)}, f32[32,4224]{1,0:T(8,128)}, u32[]{:S(2)}, u32[]{:S(2)}) collective-permute-start(f32[32,4224]{1,0:T(8,128)S(1)} %copy.56), channel_id=1, source_target_pairs={{0,4},{1,5},{2,6},{3,7},{4,0},{5,1},{6,2},{7,3},{8,12},{9,13},{10,... | collective-permute-start | bytes 1622024 | tf_op jit(solution)/shard_map/ppermute | solution.py:51
  248.3 25.3 %copy-start.8 = (f32[32,4096]{1,0:T(8,128)}, f32[32,4096]{1,0:T(8,128)S(1)}, u32[]{:S(2)}) copy-start(f32[32,4096]{1,0:T(8,128)S(1)} %fusion.6) | copy-start | bytes 1572868
  250.4 4.8 %collective-permute-start.18 = (f32[512,32]{0,1:T(8,128)S(1)}, f32[512,32]{0,1:T(8,128)S(1)}, u32[]{:S(2)}, u32[]{:S(2)}) collective-permute-start(f32[512,32]{0,1:T(8,128)S(1)} %fusion.17), channel_id=1, source_target_pairs={{0,32},{32,0},{1,33},{33,1},{2,34},{34,2},{3,35},{35,3},{4,36},{36... | collective-permute-start | bytes 196616 | tf_op jit(solution)/shard_map/ppermute | solution.py:17
  264.1 9.4 %collective-permute-start.19 = (f32[32,4224]{1,0:T(8,128)S(1)}, f32[32,4224]{1,0:T(8,128)S(1)}, u32[]{:S(2)}, u32[]{:S(2)}) collective-permute-start(f32[32,4224]{1,0:T(8,128)S(1)} %select_maximum_fusion), channel_id=1, source_target_pairs={{0,32},{32,0},{1,33},{33,1},{2,34},{34,2},{3,35},{35,3},{4,36},{36... | collective-permute-start | bytes 1622024 | tf_op jit(solution)/shard_map/ppermute | solution.py:17
  273.6 9.4 %collective-permute-start.20 = (f32[32,4224]{1,0:T(8,128)S(1)}, f32[32,4224]{1,0:T(8,128)S(1)}, u32[]{:S(2)}, u32[]{:S(2)}) collective-permute-start(f32[32,4224]{1,0:T(8,128)S(1)} %fusion.55), channel_id=1, source_target_pairs={{0,1},{1,0},{2,3},{3,2},{4,5},{5,4},{6,7},{7,6},{8,9},{9,8},{10,11... | collective-permute-start | bytes 1622024 | tf_op jit(solution)/shard_map/ppermute | solution.py:51
  287.6 14.6 %copy-start.3 = (f32[32,4224]{0,1:T(8,128)}, f32[32,4224]{0,1:T(8,128)S(1)}, u32[]{:S(2)}) copy-start(f32[32,4224]{0,1:T(8,128)S(1)} %add.155) | copy-start | bytes 1622020
  289.1 13.1 %collective-permute-start.21 = (f32[32,4224]{1,0:T(8,128)}, f32[32,4224]{1,0:T(8,128)S(1)}, u32[]{:S(2)}, u32[]{:S(2)}) collective-permute-start(f32[32,4224]{1,0:T(8,128)} %copy.61), channel_id=1, source_target_pairs={{0,2},{1,3},{2,0},{3,1},{4,6},{5,7},{6,4},{7,5},{8,10},{9,11},{10,... | collective-permute-start | bytes 1622024 | tf_op jit(solution)/shard_map/ppermute | solution.py:51
  308.1 18.2 %collective-permute-start.22 = (f32[32,4224]{1,0:T(8,128)}, f32[32,4224]{1,0:T(8,128)}, u32[]{:S(2)}, u32[]{:S(2)}) collective-permute-start(f32[32,4224]{1,0:T(8,128)} %copy.63), channel_id=1, source_target_pairs={{0,4},{1,5},{2,6},{3,7},{4,0},{5,1},{6,2},{7,3},{8,12},{9,13},{10,... | collective-permute-start | bytes 1622024 | tf_op jit(solution)/shard_map/ppermute | solution.py:51
  339.9 11.9 %copy-start.1 = (bf16[1,1024,512]{2,1,0:T(8,128)(2,1)S(1)}, bf16[1,1024,512]{2,1,0:T(8,128)(2,1)}, u32[]{:S(2)}) copy-start(bf16[1,1024,512]{2,1,0:T(8,128)(2,1)} %param.11) | copy-start | bytes 3145732
  (3 other events, 4.0 us)

commit v3 on v2

--- a/solution.py
+++ b/solution.py
@@ -53,6 +53,24 @@
     return parts
 
 
+def halving_allreduce(buf, pair_axis, count):
+    t = lax.axis_index("tp")
+    stages = [(pair_axis, lax.axis_index(pair_axis), [(0, 1), (1, 0)])]
+    bit = 1
+    while bit < count:
+        stages.append(("tp", (t // bit) % 2, tp_perm(count, lambda u, b=bit: u ^ b)))
+        bit *= 2
+    for axis, v, perm in stages:
+        half = buf.shape[0] // 2
+        keep = lax.dynamic_slice_in_dim(buf, v * half, half, 0)
+        give = lax.dynamic_slice_in_dim(buf, (1 - v) * half, half, 0)
+        buf = keep + lax.ppermute(give, axis, perm)
+    for axis, v, perm in reversed(stages):
+        other = lax.ppermute(buf, axis, perm)
+        buf = jnp.where(v == 1, jnp.concatenate([other, buf]), jnp.concatenate([buf, other]))
+    return buf
+
+
 def shards(acts, weights, cotangent, start_factors):
     scale = D ** (-0.5)
     count = lax.axis_size("tp")
@@ -75,32 +93,33 @@
     grad = lax.dot_general(rel, grad_rel, (((0,), (0,)), ((), ())), preferred_element_type=F32)
     current = weight_part.astype(F32) - 0.5 * scale * grad
     side = lax.dot_general(current, start_factors, (((0,), (0,)), ((), ())), precision=FAST)
+    pieces = 2 * count
+    current3 = current.reshape(pieces, -1, current.shape[1])
+    factors3 = start_factors.reshape(pieces, -1, start_factors.shape[1])
     backs, orthos = [], []
     eye = jnp.eye(start_factors.shape[1], dtype=F32)
     for step in range(STEPS):
         axis = f"b{step}"
         diff = side - swap(side, axis)
         gram = jnp.dot(diff.T, diff, precision=HIGH)
-        mixed = lax.dot_general(diff, current, (((0,), (1,)), ((), ())), precision=FAST)
-        for back_t, ortho_t in zip(backs, orthos):
+        mixed = jnp.einsum("gio,ok->gki", current3, diff, precision=FAST)
+        for back3, ortho_t in zip(backs, orthos):
             inner = jnp.dot(ortho_t, diff, precision=HIGH)
-            mixed = mixed - 0.5 * lax.dot_general(inner, back_t, (((0,), (0,)), ((), ())), precision=HIGH)
-        width = mixed.shape[0]
-        packed = jnp.concatenate([jnp.pad(gram, ((0, 0), (0, 128 - width))), mixed], axis=1)
-        (packed,) = allreduce([packed], axis, count)
-        gram, mixed = packed[:, :width], packed[:, 128:]
+            mixed = mixed - 0.5 * jnp.einsum("lk,gli->gki", inner, back3, precision=HIGH)
+        (gram,) = allreduce([gram], axis, count)
+        mixed = halving_allreduce(mixed, axis, count)
         lower = jnp.linalg.cholesky(0.5 * gram)
         inv = jax.scipy.linalg.solve_triangular(lower, eye, lower=True)
-        back_t = jnp.dot(inv, mixed, precision=HIGH)
+        back3 = jnp.einsum("kl,gli->gki", inv, mixed, precision=HIGH)
         ortho_t = jnp.dot(inv, diff.T, precision=HIGH)
-        backs.append(back_t)
+        backs.append(back3)
         orthos.append(ortho_t)
         if step + 1 < STEPS:
-            proj = jnp.dot(back_t, start_factors, precision=HIGH)
+            proj = jnp.einsum("gki,gil->kl", back3, factors3, precision=HIGH)
             side = side - 0.5 * lax.dot_general(ortho_t, proj, (((0,), (0,)), ((), ())), precision=HIGH)
-    back_all = jnp.concatenate(backs)
+    back_all = jnp.concatenate(backs, axis=1)
     ortho_all = jnp.concatenate(orthos)
-    update = lax.dot_general(back_all, ortho_all, (((0,), (0,)), ((), ())), precision=FAST)
+    update = jnp.einsum("gki,ko->gio", back_all, ortho_all, precision=FAST).reshape(current.shape)
     new = current - 0.5 * update
     return (projected, new.astype(jnp.bfloat16)[None])
 

time: 357 us -> 285 us (0.80)
  waiting for transfers between devices: 160 us -> 123 us
  local copies, waits for them, and re-layouts: 48.3 us -> 12 us
  starting transfers between devices: 35.2 us -> 62.4 us
  other arithmetic: 45.6 us -> 32.2 us
  matrix products: 61.2 us -> 49.5 us
    ppermute x9, waiting for transfers between devices: 80.2 us -> 12.4 us  [allreduce(): parts = [p + lax.ppermute(p, 'tp', perm) for p in parts]]
    ppermute x0 -> x24, waiting for transfers between devices: none -> 47.1 us  [the longest x12 33.8 us: halving_allreduce(): other = lax.ppermute(buf, axis, perm)]
    ppermute x0 -> x24, starting transfers between devices: none -> 26.4 us  [the longest x12 14.7 us: halving_allreduce(): other = lax.ppermute(buf, axis, perm)]
    add x9 -> x6, other arithmetic: 21.7 us -> 0.03 us  [allreduce(): parts = [p + lax.ppermute(p, 'tp', perm) for p in parts]]
    ppermute x9 -> x0, local copies, waits for them, and re-layouts: 20.4 us -> none  [allreduce(): parts = [p + lax.ppermute(p, 'tp', perm) for p in parts]]
    ppermute x6, waiting for transfers between devices: 32.2 us -> 14.8 us  [swap(): return lax.ppermute(block, axis, [(0, 1), (1, 0)])]
    add x9 -> x0, local copies, waits for them, and re-layouts: 16.1 us -> none  [the longest x6 10.1 us: allreduce(): parts = [p + lax.ppermute(p, 'tp', perm) for p in parts]]
    dot_general x12, matrix products: 41.1 us -> 31.5 us  [the longest x3 21.2 us: shards(): mixed = jnp.einsum('gio,ok->gki', current3, diff, precision=FAST)]
  transfers between devices with their start and end apart: 23 -> 47, of which waited for: 18 -> 37; matrix products, arithmetic and copies ran while one was open for 7% -> 17% of each run, Pallas kernels for 0% -> 0%
where the time goes in v3:
time: 285 us; the launch traced here: 280 us
  waiting for transfers between devices  123 us (43%)
  starting transfers between devices  62.4 us (22%)
  matrix products  49.5 us (17%)
  other arithmetic  32.2 us (11%)
  local copies, waits for them, and re-layouts  12 us (4%)
    ppermute x12, waiting for transfers between devices, halving_allreduce(): other = lax.ppermute(buf, axis, perm)  33.8 us
    dot_general x3, matrix products, shards(): mixed = jnp.einsum('gio,ok->gki', current3, diff, precision=FAST)  21.2 us
    ppermute x1, waiting for transfers between devices, gather_tokens(): a_p = lax.ppermute(own, 'tp', shift(-1))  20.5 us
    ppermute x1, waiting for transfers between devices, gather_tokens(): b_p = lax.ppermute(a_p, 'tp', shift(-1))  19.5 us
    ppermute x6, waiting for transfers between devices, swap(): return lax.ppermute(block, axis, [(0, 1), (1, 0)])  14.8 us
    ppermute x12, starting transfers between devices, halving_allreduce(): other = lax.ppermute(buf, axis, perm)  14.7 us
    ppermute x12, waiting for transfers between devices, halving_allreduce(): buf = keep + lax.ppermute(give, axis, perm)  13.2 us
    ppermute x9, starting transfers between devices, allreduce(): parts = [p + lax.ppermute(p, 'tp', perm) for p in parts]  13.1 us
  transfers between devices with their start and end apart: 47, of which 37 were waited for; matrix products, arithmetic and copies ran while one was open for 17% of the time, Pallas kernels for 0%

profile of v3, /device:TPU:16, one launch (start us, length us, event | category | flops | bytes accessed | tf_op | source)
XLA Modules:
  0.0 280.4 jit_solution(9782810663007792906)
XLA Ops:
  2.0 2.8 collective-permute-start.1
  6.7 20.5 %collective-permute-done.1 = bf16[128,4096]{1,0:T(8,128)(2,1)} collective-permute-done((bf16[128,4096]{1,0:T(8,128)(2,1)}, bf16[128,4096]{1,0:T(8,128)(2,1)}, u32[]{:S(2)}, u32[]{:S(2)}) %collective-permute-start.1) | collective-permute-done | bytes 1048608 | tf_op jit(solution)/shard_map/ppermute | solution.py:37
  28.0 3.7 %collective-permute-start.3 = (bf16[128,4096]{1,0:T(8,128)(2,1)}, bf16[128,4096]{1,0:T(8,128)(2,1)S(1)}, u32[]{:S(2)}, u32[]{:S(2)}) collective-permute-start(bf16[128,4096]{1,0:T(8,128)(2,1)} %collective-permute-done.1), channel_id=1, source_target_pairs={{0,6},{1,7},{2,0},{3,1},{4,2},{5,3},{6,4},{7,5},{8,14},{9,15},{10,... | collective-permute-start | bytes 3145736 | tf_op jit(solution)/shard_map/ppermute | solution.py:39
  33.5 19.5 %collective-permute-done.3 = bf16[128,4096]{1,0:T(8,128)(2,1)S(1)} collective-permute-done((bf16[128,4096]{1,0:T(8,128)(2,1)}, bf16[128,4096]{1,0:T(8,128)(2,1)S(1)}, u32[]{:S(2)}, u32[]{:S(2)}) %collective-permute-start.3) | collective-permute-done | bytes 1048608 | tf_op jit(solution)/shard_map/ppermute | solution.py:39
  54.4 4.2 %collective-permute-start.5 = (bf16[64,4096]{1,0:T(8,128)(2,1)S(1)}, bf16[64,4096]{1,0:T(8,128)(2,1)S(1)}, u32[]{:S(2)}, u32[]{:S(2)}) collective-permute-start(bf16[64,4096]{1,0:T(8,128)(2,1)S(1)} %slice.21), channel_id=1, source_target_pairs={{0,6},{1,7},{2,0},{3,1},{4,2},{5,3},{6,4},{7,5},{8,14},{9,15},{10,... | collective-permute-start | bytes 1572872 | tf_op jit(solution)/shard_map/ppermute | solution.py:42
  58.8 5.7 %collective-permute-done.4 = bf16[64,4096]{1,0:T(8,128)(2,1)S(1)} collective-permute-done((bf16[64,4096]{1,0:T(8,128)(2,1)S(1)}, bf16[64,4096]{1,0:T(8,128)(2,1)S(1)}, u32[]{:S(2)}, u32[]{:S(2)}) %collective-permute-start.4) | collective-permute-done | bytes 524320 | tf_op jit(solution)/shard_map/ppermute | solution.py:41
  64.5 2.7 collective-permute-done.5
  68.7 4.7 %multiply_subtract_fusion = f32[4096,512]{1,0:T(8,128)S(1)} fusion(bf16[1024,4096]{1,0:T(8,128)(2,1)S(1)} %constant_dynamic-update-slice_fusion, bf16[1024,512]{1,0:T(8,128)(2,1)S(1)} %bitcast.156, bf16[1,4096,512]{2,1,0:T(8,128)(2,1)S(1)} %copy-done.5), kind=kOutput, calls=%fused_computation.5 | convolution fusion | flops 4301258752 | bytes 22020096 | tf_op jit(solution)/shard_map/dot_general | solution.py:93
  73.4 3.3 %copy-done.1 = f32[4096,512]{1,0:T(8,128)} copy-done((f32[4096,512]{1,0:T(8,128)}, f32[4096,512]{1,0:T(8,128)S(1)}, u32[]{:S(2)}) %copy-start.1) | copy-done | bytes 8388632
  80.5 7.1 %fusion.46 = f32[32,16,256]{2,0,1:T(8,128)S(1)} fusion(f32[16,256,512]{2,1,0:T(8,128)} %bitcast.149, f32[512,32]{0,1:T(8,128)S(1)} %sub.80), kind=kOutput, calls=%fused_computation.88 | convolution fusion | flops 402653184 | bytes 8978432 | tf_op jit(solution)/shard_map/gio,ok->gki/dot_general | solution.py:105
  93.0 2.5 collective-permute-done.18
  95.6 3.7 %collective-permute-done.19 = f32[32,32]{0,1:T(8,128)S(1)} collective-permute-done((f32[32,32]{0,1:T(8,128)S(1)}, f32[32,32]{0,1:T(8,128)S(1)}, u32[]{:S(2)}, u32[]{:S(2)}) %collective-permute-start.19) | collective-permute-done | bytes 4128 | tf_op jit(solution)/shard_map/ppermute | solution.py:51
  99.2 3.1 %collective-permute-start.20 = (f32[32,32]{0,1:T(8,128)S(1)}, f32[32,32]{0,1:T(8,128)S(1)}, u32[]{:S(2)}, u32[]{:S(2)}) collective-permute-start(f32[32,32]{0,1:T(8,128)S(1)} %add.256), channel_id=1, source_target_pairs={{0,4},{1,5},{2,6},{3,7},{4,0},{5,1},{6,2},{7,3},{8,12},{9,13},{10,... | collective-permute-start | bytes 12296 | tf_op jit(solution)/shard_map/ppermute | solution.py:51
  107.8 2.9 %cholesky.59 = f32[32,32]{1,0:T(8,128)S(1)} custom-call(f32[32,32]{1,0:T(8,128)S(1)} %fusion.65), custom_call_target="Cholesky" | custom-call | tf_op jit(solution)/shard_map/jit(cholesky)/cholesky | solution.py:111
  113.5 4.6 %collective-permute-done.13 = f32[1,32,256]{2,1,0:T(8,128)S(1)} collective-permute-done((f32[1,32,256]{2,1,0:T(8,128)S(1)}, f32[1,32,256]{2,1,0:T(8,128)S(1)}, u32[]{:S(2)}, u32[]{:S(2)}) %collective-permute-start.13) | collective-permute-done | bytes 32800 | tf_op jit(solution)/shard_map/ppermute | solution.py:69
  131.1 5.4 %collective-permute-done.21 = f32[512,32]{0,1:T(8,128)S(1)} collective-permute-done((f32[512,32]{0,1:T(8,128)S(1)}, f32[512,32]{0,1:T(8,128)S(1)}, u32[]{:S(2)}, u32[]{:S(2)}) %collective-permute-start.21) | collective-permute-done | bytes 65568 | tf_op jit(solution)/shard_map/ppermute | solution.py:17
  137.4 7.1 %fusion.13 = f32[16,32,256]{2,1,0:T(8,128)S(1)} fusion(f32[16,32,256]{2,1,0:T(8,128)S(1)} %fusion.12, f32[16,256,512]{2,1,0:T(8,128)} %bitcast.150, f32[512,32]{0,1:T(8,128)S(1)} %sub.86), kind=kOutput, calls=%fused_computation.26 | convolution fusion | flops 402784256 | bytes 9502720 | tf_op jit(solution)/shard_map/gio,ok->gki/dot_general | solution.py:105
  145.0 3.3 %collective-permute-start.30 = (f32[32,32]{0,1:T(8,128)S(1)}, f32[32,32]{0,1:T(8,128)S(1)}, u32[]{:S(2)}, u32[]{:S(2)}) collective-permute-start(f32[32,32]{0,1:T(8,128)S(1)} %fusion.86), channel_id=1, source_target_pairs={{0,16},{16,0},{1,17},{17,1},{2,18},{18,2},{3,19},{19,3},{4,20},{20... | collective-permute-start | bytes 12296 | tf_op jit(solution)/shard_map/ppermute | solution.py:17
  149.0 4.7 %collective-permute-done.30 = f32[32,32]{0,1:T(8,128)S(1)} collective-permute-done((f32[32,32]{0,1:T(8,128)S(1)}, f32[32,32]{0,1:T(8,128)S(1)}, u32[]{:S(2)}, u32[]{:S(2)}) %collective-permute-start.30) | collective-permute-done | bytes 4128 | tf_op jit(solution)/shard_map/ppermute | solution.py:17
  170.4 2.9 %cholesky.70 = f32[32,32]{1,0:T(8,128)S(1)} custom-call(f32[32,32]{1,0:T(8,128)S(1)} %fusion.62), custom_call_target="Cholesky" | custom-call | tf_op jit(solution)/shard_map/jit(cholesky)/cholesky | solution.py:111
  175.8 3.6 %collective-permute-done.26 = f32[1,32,256]{2,1,0:T(8,128)S(1)} collective-permute-done((f32[1,32,256]{2,1,0:T(8,128)S(1)}, f32[1,32,256]{2,1,0:T(8,128)S(1)}, u32[]{:S(2)}, u32[]{:S(2)}) %collective-permute-start.26) | collective-permute-done | bytes 32800 | tf_op jit(solution)/shard_map/ppermute | solution.py:69
  180.6 3.2 %collective-permute-done.27 = f32[2,32,256]{2,1,0:T(8,128)S(1)} collective-permute-done((f32[2,32,256]{2,1,0:T(8,128)S(1)}, f32[2,32,256]{2,1,0:T(8,128)S(1)}, u32[]{:S(2)}, u32[]{:S(2)}) %collective-permute-start.27) | collective-permute-done | bytes 65568 | tf_op jit(solution)/shard_map/ppermute | solution.py:69
  185.6 2.4 custom-call.8
  190.1 6.7 %collective-permute-done.29 = f32[8,32,256]{2,1,0:T(8,128)S(1)} collective-permute-done((f32[8,32,256]{2,1,0:T(8,128)S(1)}, f32[8,32,256]{2,1,0:T(8,128)S(1)}, u32[]{:S(2)}, u32[]{:S(2)}) %collective-permute-start.29) | collective-permute-done | bytes 262176 | tf_op jit(solution)/shard_map/ppermute | solution.py:69
  206.8 7.1 %fusion.15 = f32[16,32,256]{2,1,0:T(8,128)S(1)} fusion(f32[16,32,256]{2,1,0:T(8,128)S(1)} %fusion.10, f32[16,32,256]{2,1,0:T(8,128)S(1)} %fusion.11, f32[16,256,512]{2,1,0:T(8,128)} %bitcast.151, f32[512,32]{0,1:T(8,128)S(1)} %sub.90), kind=kOutput, calls=%fused_computation.28 | convolution fusion | flops 402915328 | bytes 10027008 | tf_op jit(solution)/shard_map/gio,ok->gki/dot_general | solution.py:105
  216.0 8.0 %multiply_convert_fusion = bf16[1024,512]{1,0:T(8,128)(2,1)} fusion(bf16[1024,4096]{1,0:T(8,128)(2,1)} %copy-done.4, bf16[1,4096,512]{2,1,0:T(8,128)(2,1)S(1)} %copy-done.6), kind=kOutput, calls=%fused_computation.9 | convolution fusion | flops 4296015872 | bytes 13631488 | tf_op jit(solution)/shard_map/dot_general | solution.py:88
  239.4 2.9 %cholesky.81 = f32[32,32]{1,0:T(8,128)S(1)} custom-call(f32[32,32]{1,0:T(8,128)S(1)} %fusion.59), custom_call_target="Cholesky" | custom-call | tf_op jit(solution)/shard_map/jit(cholesky)/cholesky | solution.py:111
  244.8 3.5 %collective-permute-done.39 = f32[1,32,256]{2,1,0:T(8,128)S(1)} collective-permute-done((f32[1,32,256]{2,1,0:T(8,128)S(1)}, f32[1,32,256]{2,1,0:T(8,128)S(1)}, u32[]{:S(2)}, u32[]{:S(2)}) %collective-permute-start.39) | collective-permute-done | bytes 32800 | tf_op jit(solution)/shard_map/ppermute | solution.py:69
  250.2 2.4 collective-permute-done.40
  260.3 4.0 %collective-permute-done.42 = f32[8,32,256]{2,1,0:T(8,128)S(1)} collective-permute-done((f32[8,32,256]{2,1,0:T(8,128)S(1)}, f32[8,32,256]{2,1,0:T(8,128)S(1)}, u32[]{:S(2)}, u32[]{:S(2)}) %collective-permute-start.42) | collective-permute-done | bytes 262176 | tf_op jit(solution)/shard_map/ppermute | solution.py:69
  265.0 5.8 %broadcast_multiply_fusion = f32[16,256,512]{2,1,0:T(8,128)} fusion(f32[16,32,256]{2,1,0:T(8,128)S(1)} %convolution_bitcast_fusion, f32[16,32,256]{2,1,0:T(8,128)S(1)} %convolution_bitcast_fusion.2, f32[16,32,256]{2,1,0:T(8,128)S(1)} %convolution_bitcast_fusion.4, f32[32,512]{1,0:T(8,128)S(1)} %fusion.89, f32[32,512]{1,0:T(8,128)S(1)} %fusion.87, ...), kind=kOutput, calls=%fused_computation.8 | convolution fusion | flops 1210941440 | bytes 10158080 | tf_op jit(solution)/shard_map/gki,ko->gio/dot_general | solution.py:122
  270.8 9.5 %fusion = bf16[4096,512]{1,0:T(8,128)(2,1)} fusion(f32[4096,512]{1,0:T(8,128)} %copy-done.1, f32[16,256,512]{2,1,0:T(8,128)} %broadcast_multiply_fusion), kind=kLoop, calls=%fused_computation.4 | loop fusion | flops 4194304 | bytes 20971520 | tf_op jit(solution)/shard_map/convert_element_type | solution.py:124
  (198 shorter events, 105.5 us)
Async XLA Ops:
  0.6 31.2 %collective-permute-start = (bf16[128,4096]{1,0:T(8,128)(2,1)}, bf16[128,4096]{1,0:T(8,128)(2,1)S(1)}, u32[]{:S(2)}, u32[]{:S(2)}) collective-permute-start(bf16[128,4096]{1,0:T(8,128)(2,1)} %bitcast.158), channel_id=1, source_target_pairs={{0,1},{1,0},{2,3},{3,2},{4,5},{5,4},{6,7},{7,6},{8,9},{9,8},{10,11... | collective-permute-start | bytes 3145736 | tf_op jit(solution)/shard_map/ppermute | solution.py:35
  2.0 25.2 %collective-permute-start.1 = (bf16[128,4096]{1,0:T(8,128)(2,1)}, bf16[128,4096]{1,0:T(8,128)(2,1)}, u32[]{:S(2)}, u32[]{:S(2)}) collective-permute-start(bf16[128,4096]{1,0:T(8,128)(2,1)} %bitcast.159), channel_id=1, source_target_pairs={{0,6},{1,7},{2,0},{3,1},{4,2},{5,3},{6,4},{7,5},{8,14},{9,15},{10,... | collective-permute-start | bytes 3145736 | tf_op jit(solution)/shard_map/ppermute | solution.py:37
  4.8 62.5 %collective-permute-start.6 = (bf16[128,4096]{1,0:T(8,128)(2,1)}, bf16[128,4096]{1,0:T(8,128)(2,1)}, u32[]{:S(2)}, u32[]{:S(2)}) collective-permute-start(bf16[128,4096]{1,0:T(8,128)(2,1)} %bitcast.160), channel_id=1, source_target_pairs={{0,2},{1,3},{2,4},{3,5},{4,6},{5,7},{6,0},{7,1},{8,10},{9,11},{10,... | collective-permute-start | bytes 3145736 | tf_op jit(solution)/shard_map/ppermute | solution.py:36
  27.2 27.2 %collective-permute-start.2 = (bf16[128,4096]{1,0:T(8,128)(2,1)}, bf16[128,4096]{1,0:T(8,128)(2,1)S(1)}, u32[]{:S(2)}, u32[]{:S(2)}) collective-permute-start(bf16[128,4096]{1,0:T(8,128)(2,1)} %collective-permute-done.1), channel_id=1, source_target_pairs={{0,1},{1,0},{2,3},{3,2},{4,5},{5,4},{6,7},{7,6},{8,9},{9,8},{10,11... | collective-permute-start | bytes 3145736 | tf_op jit(solution)/shard_map/ppermute | solution.py:40
  28.0 25.0 %collective-permute-start.3 = (bf16[128,4096]{1,0:T(8,128)(2,1)}, bf16[128,4096]{1,0:T(8,128)(2,1)S(1)}, u32[]{:S(2)}, u32[]{:S(2)}) collective-permute-start(bf16[128,4096]{1,0:T(8,128)(2,1)} %collective-permute-done.1), channel_id=1, source_target_pairs={{0,6},{1,7},{2,0},{3,1},{4,2},{5,3},{6,4},{7,5},{8,14},{9,15},{10,... | collective-permute-start | bytes 3145736 | tf_op jit(solution)/shard_map/ppermute | solution.py:39
  31.9 36.8 %collective-permute-start.7 = (bf16[128,4096]{1,0:T(8,128)(2,1)S(1)}, bf16[128,4096]{1,0:T(8,128)(2,1)S(1)}, u32[]{:S(2)}, u32[]{:S(2)}) collective-permute-start(bf16[128,4096]{1,0:T(8,128)(2,1)S(1)} %collective-permute-done), channel_id=1, source_target_pairs={{0,2},{1,3},{2,4},{3,5},{4,6},{5,7},{6,0},{7,1},{8,10},{9,11},{10,... | collective-permute-start | bytes 3145736 | tf_op jit(solution)/shard_map/ppermute | solution.py:38
  53.0 11.5 %collective-permute-start.4 = (bf16[64,4096]{1,0:T(8,128)(2,1)S(1)}, bf16[64,4096]{1,0:T(8,128)(2,1)S(1)}, u32[]{:S(2)}, u32[]{:S(2)}) collective-permute-start(bf16[64,4096]{1,0:T(8,128)(2,1)S(1)} %slice.20), channel_id=1, source_target_pairs={{0,1},{1,0},{2,3},{3,2},{4,5},{5,4},{6,7},{7,6},{8,9},{9,8},{10,11... | collective-permute-start | bytes 1572872 | tf_op jit(solution)/shard_map/ppermute | solution.py:41
  54.4 12.8 %collective-permute-start.5 = (bf16[64,4096]{1,0:T(8,128)(2,1)S(1)}, bf16[64,4096]{1,0:T(8,128)(2,1)S(1)}, u32[]{:S(2)}, u32[]{:S(2)}) collective-permute-start(bf16[64,4096]{1,0:T(8,128)(2,1)S(1)} %slice.21), channel_id=1, source_target_pairs={{0,6},{1,7},{2,0},{3,1},{4,2},{5,3},{6,4},{7,5},{8,14},{9,15},{10,... | collective-permute-start | bytes 1572872 | tf_op jit(solution)/shard_map/ppermute | solution.py:42
  89.2 13.1 %collective-permute-start.10 = (f32[4,32,256]{2,1,0:T(8,128)S(1)}, f32[4,32,256]{2,1,0:T(8,128)S(1)}, u32[]{:S(2)}, u32[]{:S(2)}) collective-permute-start(f32[4,32,256]{2,1,0:T(8,128)S(1)} %constant_dynamic-slice_fusion.10), channel_id=1, source_target_pairs={{0,1},{1,0},{2,3},{3,2},{4,5},{5,4},{6,7},{7,6},{8,9},{9,8},{10,11... | collective-permute-start | bytes 393224 | tf_op jit(solution)/shard_map/ppermute | solution.py:67
  99.2 5.2 %collective-permute-start.20 = (f32[32,32]{0,1:T(8,128)S(1)}, f32[32,32]{0,1:T(8,128)S(1)}, u32[]{:S(2)}, u32[]{:S(2)}) collective-permute-start(f32[32,32]{0,1:T(8,128)S(1)} %add.256), channel_id=1, source_target_pairs={{0,4},{1,5},{2,6},{3,7},{4,0},{5,1},{6,2},{7,3},{8,12},{9,13},{10,... | collective-permute-start | bytes 12296 | tf_op jit(solution)/shard_map/ppermute | solution.py:51
  106.8 5.5 %collective-permute-start.12 = (f32[1,32,256]{2,1,0:T(8,128)S(1)}, f32[1,32,256]{2,1,0:T(8,128)S(1)}, u32[]{:S(2)}, u32[]{:S(2)}) collective-permute-start(f32[1,32,256]{2,1,0:T(8,128)S(1)} %constant_dynamic-slice_fusion.8), channel_id=1, source_target_pairs={{0,4},{1,5},{2,6},{3,7},{4,0},{5,1},{6,2},{7,3},{8,12},{9,13},{10,... | collective-permute-start | bytes 98312 | tf_op jit(solution)/shard_map/ppermute | solution.py:67
  112.3 5.8 %collective-permute-start.13 = (f32[1,32,256]{2,1,0:T(8,128)S(1)}, f32[1,32,256]{2,1,0:T(8,128)S(1)}, u32[]{:S(2)}, u32[]{:S(2)}) collective-permute-start(f32[1,32,256]{2,1,0:T(8,128)S(1)} %dynamic-slice_add_fusion.10), channel_id=1, source_target_pairs={{0,4},{1,5},{2,6},{3,7},{4,0},{5,1},{6,2},{7,3},{8,12},{9,13},{10,... | collective-permute-start | bytes 98312 | tf_op jit(solution)/shard_map/ppermute | solution.py:69
  122.4 5.1 %collective-permute-start.15 = (f32[4,32,256]{2,1,0:T(8,128)S(1)}, f32[4,32,256]{2,1,0:T(8,128)S(1)}, u32[]{:S(2)}, u32[]{:S(2)}) collective-permute-start(f32[4,32,256]{2,1,0:T(8,128)S(1)} %maximum_select_fusion.9), channel_id=1, source_target_pairs={{0,1},{1,0},{2,3},{3,2},{4,5},{5,4},{6,7},{7,6},{8,9},{9,8},{10,11... | collective-permute-start | bytes 393224 | tf_op jit(solution)/shard_map/ppermute | solution.py:69
  130.6 5.9 %collective-permute-start.21 = (f32[512,32]{0,1:T(8,128)S(1)}, f32[512,32]{0,1:T(8,128)S(1)}, u32[]{:S(2)}, u32[]{:S(2)}) collective-permute-start(f32[512,32]{0,1:T(8,128)S(1)} %fusion.17), channel_id=1, source_target_pairs={{0,16},{16,0},{1,17},{17,1},{2,18},{18,2},{3,19},{19,3},{4,20},{20... | collective-permute-start | bytes 196616 | tf_op jit(solution)/shard_map/ppermute | solution.py:17
  144.5 14.4 %collective-permute-start.22 = (f32[8,32,256]{2,1,0:T(8,128)S(1)}, f32[8,32,256]{2,1,0:T(8,128)S(1)}, u32[]{:S(2)}, u32[]{:S(2)}) collective-permute-start(f32[8,32,256]{2,1,0:T(8,128)S(1)} %constant_dynamic-slice_fusion.7), channel_id=1, source_target_pairs={{0,16},{16,0},{1,17},{17,1},{2,18},{18,2},{3,19},{19,3},{4,20},{20... | collective-permute-start | bytes 786440 | tf_op jit(solution)/shard_map/ppermute | solution.py:67
  145.0 8.6 %collective-permute-start.30 = (f32[32,32]{0,1:T(8,128)S(1)}, f32[32,32]{0,1:T(8,128)S(1)}, u32[]{:S(2)}, u32[]{:S(2)}) collective-permute-start(f32[32,32]{0,1:T(8,128)S(1)} %fusion.86), channel_id=1, source_target_pairs={{0,16},{16,0},{1,17},{17,1},{2,18},{18,2},{3,19},{19,3},{4,20},{20... | collective-permute-start | bytes 12296 | tf_op jit(solution)/shard_map/ppermute | solution.py:17
  159.0 5.1 %collective-permute-start.23 = (f32[4,32,256]{2,1,0:T(8,128)S(1)}, f32[4,32,256]{2,1,0:T(8,128)S(1)}, u32[]{:S(2)}, u32[]{:S(2)}) collective-permute-start(f32[4,32,256]{2,1,0:T(8,128)S(1)} %constant_dynamic-slice_fusion.6), channel_id=1, source_target_pairs={{0,1},{1,0},{2,3},{3,2},{4,5},{5,4},{6,7},{7,6},{8,9},{9,8},{10,11... | collective-permute-start | bytes 393224 | tf_op jit(solution)/shard_map/ppermute | solution.py:67
  161.2 5.2 %collective-permute-start.33 = (f32[32,32]{0,1:T(8,128)S(1)}, f32[32,32]{0,1:T(8,128)S(1)}, u32[]{:S(2)}, u32[]{:S(2)}) collective-permute-start(f32[32,32]{0,1:T(8,128)S(1)} %add.266), channel_id=1, source_target_pairs={{0,4},{1,5},{2,6},{3,7},{4,0},{5,1},{6,2},{7,3},{8,12},{9,13},{10,... | collective-permute-start | bytes 12296 | tf_op jit(solution)/shard_map/ppermute | solution.py:51
  168.5 5.5 %collective-permute-start.25 = (f32[1,32,256]{2,1,0:T(8,128)S(1)}, f32[1,32,256]{2,1,0:T(8,128)S(1)}, u32[]{:S(2)}, u32[]{:S(2)}) collective-permute-start(f32[1,32,256]{2,1,0:T(8,128)S(1)} %constant_dynamic-slice_fusion.4), channel_id=1, source_target_pairs={{0,4},{1,5},{2,6},{3,7},{4,0},{5,1},{6,2},{7,3},{8,12},{9,13},{10,... | collective-permute-start | bytes 98312 | tf_op jit(solution)/shard_map/ppermute | solution.py:67
  174.0 5.4 %collective-permute-start.26 = (f32[1,32,256]{2,1,0:T(8,128)S(1)}, f32[1,32,256]{2,1,0:T(8,128)S(1)}, u32[]{:S(2)}, u32[]{:S(2)}) collective-permute-start(f32[1,32,256]{2,1,0:T(8,128)S(1)} %dynamic-slice_add_fusion.9), channel_id=1, source_target_pairs={{0,4},{1,5},{2,6},{3,7},{4,0},{5,1},{6,2},{7,3},{8,12},{9,13},{10,... | collective-permute-start | bytes 98312 | tf_op jit(solution)/shard_map/ppermute | solution.py:69
  183.8 5.1 %collective-permute-start.28 = (f32[4,32,256]{2,1,0:T(8,128)S(1)}, f32[4,32,256]{2,1,0:T(8,128)S(1)}, u32[]{:S(2)}, u32[]{:S(2)}) collective-permute-start(f32[4,32,256]{2,1,0:T(8,128)S(1)} %maximum_select_fusion.10), channel_id=1, source_target_pairs={{0,1},{1,0},{2,3},{3,2},{4,5},{5,4},{6,7},{7,6},{8,9},{9,8},{10,11... | collective-permute-start | bytes 393224 | tf_op jit(solution)/shard_map/ppermute | solution.py:69
  188.9 8.0 %collective-permute-start.29 = (f32[8,32,256]{2,1,0:T(8,128)S(1)}, f32[8,32,256]{2,1,0:T(8,128)S(1)}, u32[]{:S(2)}, u32[]{:S(2)}) collective-permute-start(f32[8,32,256]{2,1,0:T(8,128)S(1)} %maximum_select_fusion.7), channel_id=1, source_target_pairs={{0,16},{16,0},{1,17},{17,1},{2,18},{18,2},{3,19},{19,3},{4,20},{20... | collective-permute-start | bytes 786440 | tf_op jit(solution)/shard_map/ppermute | solution.py:69
  198.3 4.4 %collective-permute-start.34 = (f32[512,32]{0,1:T(8,128)S(1)}, f32[512,32]{0,1:T(8,128)S(1)}, u32[]{:S(2)}, u32[]{:S(2)}) collective-permute-start(f32[512,32]{0,1:T(8,128)S(1)} %fusion.16), channel_id=1, source_target_pairs={{0,32},{32,0},{1,33},{33,1},{2,34},{34,2},{3,35},{35,3},{4,36},{36... | collective-permute-start | bytes 196616 | tf_op jit(solution)/shard_map/ppermute | solution.py:17
  204.4 10.4 %collective-permute-start.43 = (f32[32,32]{0,1:T(8,128)S(1)}, f32[32,32]{0,1:T(8,128)S(1)}, u32[]{:S(2)}, u32[]{:S(2)}) collective-permute-start(f32[32,32]{0,1:T(8,128)S(1)} %fusion.88), channel_id=1, source_target_pairs={{0,32},{32,0},{1,33},{33,1},{2,34},{34,2},{3,35},{35,3},{4,36},{36... | collective-permute-start | bytes 12296 | tf_op jit(solution)/shard_map/ppermute | solution.py:17
  214.7 12.1 %collective-permute-start.35 = (f32[8,32,256]{2,1,0:T(8,128)}, f32[8,32,256]{2,1,0:T(8,128)}, u32[]{:S(2)}, u32[]{:S(2)}) collective-permute-start(f32[8,32,256]{2,1,0:T(8,128)} %constant_dynamic-slice_fusion.3), channel_id=1, source_target_pairs={{0,32},{32,0},{1,33},{33,1},{2,34},{34,2},{3,35},{35,3},{4,36},{36... | collective-permute-start | bytes 786440 | tf_op jit(solution)/shard_map/ppermute | solution.py:67
  214.8 11.0 %collective-permute-start.44 = (f32[32,32]{0,1:T(8,128)S(1)}, f32[32,32]{0,1:T(8,128)S(1)}, u32[]{:S(2)}, u32[]{:S(2)}) collective-permute-start(f32[32,32]{0,1:T(8,128)S(1)} %add.274), channel_id=1, source_target_pairs={{0,1},{1,0},{2,3},{3,2},{4,5},{5,4},{6,7},{7,6},{8,9},{9,8},{10,11... | collective-permute-start | bytes 12296 | tf_op jit(solution)/shard_map/ppermute | solution.py:51
  227.9 5.1 %collective-permute-start.36 = (f32[4,32,256]{2,1,0:T(8,128)S(1)}, f32[4,32,256]{2,1,0:T(8,128)S(1)}, u32[]{:S(2)}, u32[]{:S(2)}) collective-permute-start(f32[4,32,256]{2,1,0:T(8,128)S(1)} %constant_dynamic-slice_fusion.2), channel_id=1, source_target_pairs={{0,1},{1,0},{2,3},{3,2},{4,5},{5,4},{6,7},{7,6},{8,9},{9,8},{10,11... | collective-permute-start | bytes 393224 | tf_op jit(solution)/shard_map/ppermute | solution.py:67
  229.7 5.3 %collective-permute-start.46 = (f32[32,32]{0,1:T(8,128)S(1)}, f32[32,32]{0,1:T(8,128)S(1)}, u32[]{:S(2)}, u32[]{:S(2)}) collective-permute-start(f32[32,32]{0,1:T(8,128)S(1)} %add.276), channel_id=1, source_target_pairs={{0,4},{1,5},{2,6},{3,7},{4,0},{5,1},{6,2},{7,3},{8,12},{9,13},{10,... | collective-permute-start | bytes 12296 | tf_op jit(solution)/shard_map/ppermute | solution.py:51
  237.4 5.5 %collective-permute-start.38 = (f32[1,32,256]{2,1,0:T(8,128)S(1)}, f32[1,32,256]{2,1,0:T(8,128)S(1)}, u32[]{:S(2)}, u32[]{:S(2)}) collective-permute-start(f32[1,32,256]{2,1,0:T(8,128)S(1)} %constant_dynamic-slice_fusion), channel_id=1, source_target_pairs={{0,4},{1,5},{2,6},{3,7},{4,0},{5,1},{6,2},{7,3},{8,12},{9,13},{10,... | collective-permute-start | bytes 98312 | tf_op jit(solution)/shard_map/ppermute | solution.py:67
  242.9 5.4 %collective-permute-start.39 = (f32[1,32,256]{2,1,0:T(8,128)S(1)}, f32[1,32,256]{2,1,0:T(8,128)S(1)}, u32[]{:S(2)}, u32[]{:S(2)}) collective-permute-start(f32[1,32,256]{2,1,0:T(8,128)S(1)} %dynamic-slice_add_fusion.8), channel_id=1, source_target_pairs={{0,4},{1,5},{2,6},{3,7},{4,0},{5,1},{6,2},{7,3},{8,12},{9,13},{10,... | collective-permute-start | bytes 98312 | tf_op jit(solution)/shard_map/ppermute | solution.py:69
  252.7 5.1 %collective-permute-start.41 = (f32[4,32,256]{2,1,0:T(8,128)S(1)}, f32[4,32,256]{2,1,0:T(8,128)S(1)}, u32[]{:S(2)}, u32[]{:S(2)}) collective-permute-start(f32[4,32,256]{2,1,0:T(8,128)S(1)} %maximum_select_fusion.11), channel_id=1, source_target_pairs={{0,1},{1,0},{2,3},{3,2},{4,5},{5,4},{6,7},{7,6},{8,9},{9,8},{10,11... | collective-permute-start | bytes 393224 | tf_op jit(solution)/shard_map/ppermute | solution.py:69
  257.8 6.6 %collective-permute-start.42 = (f32[8,32,256]{2,1,0:T(8,128)S(1)}, f32[8,32,256]{2,1,0:T(8,128)S(1)}, u32[]{:S(2)}, u32[]{:S(2)}) collective-permute-start(f32[8,32,256]{2,1,0:T(8,128)S(1)} %maximum_select_fusion.8), channel_id=1, source_target_pairs={{0,32},{32,0},{1,33},{33,1},{2,34},{34,2},{3,35},{35,3},{4,36},{36... | collective-permute-start | bytes 786440 | tf_op jit(solution)/shard_map/ppermute | solution.py:69
  (22 other events, 145.9 us)
